TPU v7x, 256 devices: a whole 4x4x8 slice. The times are simulated.
256 devices in a mesh: ctx: 32 (over y, x, core), head: 8 (over z).
Axes of the slice: x: 4, y: 4, z: 8, core: 2. Of those that a mesh axis runs over, the one named last changes fastest.
Arguments:
- queries: bfloat16 [8192, 4096], P('ctx', 'head'), may hold values from -6 to 6
- key_rows: bfloat16 [8192, 4096], P('ctx', 'head'), may hold values from -6 to 6
- values: bfloat16 [8192, 4096], P('ctx', 'head'), may hold values from -6 to 6
- log_decay: float32 [8192, 32], P('ctx', 'head'), may hold values from 0 to 1, as said below
- head_gain: bfloat16 [4096], P('head'), may hold values from 0.099609375 to 1.8984375
- out_weight: bfloat16 [3072, 4096], P('ctx', 'head'), may hold values from -0.09375 to 0.09375
- residual: bfloat16 [8192, 3072], P('ctx', 'head'), may hold values from -6 to 6
- norm_gain: bfloat16 [3072], P('head'), may hold values from 0.099609375 to 1.8984375
- router: bfloat16 [3072, 32], replicated, may hold values from -0.21875 to 0.21875
- expert_ids: int32 [8192, 2], P('ctx'), may hold values from 0 to 31, all different within a row; in each aligned block of 256 rows (0 to 255, 256 to 511, ...) at most 24 rows name the same one
- gate_weight: bfloat16 [32, 3072, 5120], P('ctx', None, 'head'), may hold values from -0.109375 to 0.109375
- up_weight: bfloat16 [32, 3072, 5120], P('ctx', None, 'head'), may hold values from -0.109375 to 0.109375
- down_weight: bfloat16 [32, 5120, 3072], P('ctx', 'head'), may hold values from -0.125 to 0.125
Outputs:
- layer_out: float32 [8192, 3072], P('ctx', 'head')
Inputs may be any that keep to these rules, and one draw needn't show every extreme that they name: `log_decay`: amounts by which a head's state decays at a position: the state is multiplied by exp(-value). `expert_ids`: each row names 2 different experts; among the rows of one block of 256 positions no expert is named more than 24 times, a bound that some block reaches.
All inputs are finite; a program needn't handle non-finite values.
Results may differ from a plain program's by a relative error of at most 0.007.
Values may be sent and summed in bfloat16 or wider, within the bound.
No kernel may reach another device: no remote copies, remote signals or barrier semaphores. Data moves between devices by JAX's collectives and lax.ppermute only.
A program may use at most 128 MiB of HBM per device.

v0:
```python
import jax
import jax.numpy as jnp
from jax import lax
from jax.sharding import PartitionSpec as P

HEAD_DIM = 128
TOP = 2


HIGH = lax.Precision.HIGHEST
EPSILON = 1e-05


def entering(value, axis, join, neutral):
    count, mine = (lax.axis_size(axis), lax.axis_index(axis))
    pieces = jax.tree.map(lambda part: lax.all_gather(part, axis), value)
    total = jax.tree.map(
        lambda part, zero: jnp.full_like(part, 0) + jnp.asarray(zero, part.dtype), value, neutral
    )

    def turn(position, total):
        longer = join(total, jax.tree.map(lambda part: part[position], pieces))
        return jax.tree.map(lambda new, old: jnp.where(position < mine, new, old), longer, total)

    return lax.fori_loop(0, count - 1, turn, total)


def chain_states(earlier, later):
    decay_early, state_early = earlier
    decay_late, state_late = later
    return (decay_early * decay_late, decay_late[:, None, None] * state_early + state_late)


def on_device(
    queries,
    key_rows,
    values,
    log_decay,
    head_gain,
    out_weight,
    residual,
    norm_gain,
    router,
    expert_ids,
    gate_weight,
    up_weight,
    down_weight,
):
    rows = queries.shape[0]
    heads_here = log_decay.shape[1]
    query_heads = queries.reshape(rows, heads_here, HEAD_DIM)
    key_heads = key_rows.reshape(rows, heads_here, HEAD_DIM)
    value_heads = values.reshape(rows, heads_here, HEAD_DIM)
    cumulative = jnp.cumsum(log_decay, axis=0)
    scores = jnp.einsum("thd,jhd->htj", query_heads, key_heads, preferred_element_type=jnp.float32)
    causal = jnp.arange(rows)[:, None] >= jnp.arange(rows)[None, :]
    gap = cumulative.T[:, :, None] - cumulative.T[:, None, :]
    weight = jnp.where(causal[None], jnp.exp(-jnp.where(causal[None], gap, 0.0)), 0.0)
    weighted = (scores * weight).astype(jnp.bfloat16)
    inner = jnp.einsum("htj,jhd->thd", weighted, value_heads, preferred_element_type=jnp.float32)
    value_wide = value_heads.astype(jnp.float32)
    tail = jnp.exp(cumulative - cumulative[-1:])
    keys_tail = key_heads.astype(jnp.float32) * tail[:, :, None]
    local_state = jnp.einsum("jhd,jhe->hde", keys_tail, value_wide, precision=HIGH)
    shard_decay = jnp.exp(-cumulative[-1])
    identity = (jnp.ones_like(shard_decay), jnp.zeros_like(local_state))
    incoming = entering((shard_decay, local_state), "ctx", chain_states, identity)[1]
    query_decayed = query_heads.astype(jnp.float32) * jnp.exp(-cumulative)[:, :, None]
    outer = jnp.einsum("thd,hde->the", query_decayed, incoming, precision=HIGH)
    mixed = inner + outer
    mean_sq = jnp.mean(mixed * mixed, axis=-1, keepdims=True)
    gain_heads = head_gain.astype(jnp.float32).reshape(heads_here, HEAD_DIM)
    normed = (
        (mixed * lax.rsqrt(mean_sq + EPSILON) * gain_heads)
        .astype(jnp.bfloat16)
        .reshape(rows, heads_here * HEAD_DIM)
    )
    partial_proj = lax.dot_general(
        normed,
        lax.all_gather(out_weight, "ctx", axis=0, tiled=True),
        (((1,), (1,)), ((), ())),
        preferred_element_type=jnp.float32,
    )
    width = residual.shape[1]
    full = width * lax.axis_size("head")
    total = lax.psum(partial_proj, "head")
    resid_full, gain_full = (
        lax.all_gather(residual, "head", axis=1, tiled=True),
        lax.all_gather(norm_gain, "head", axis=0, tiled=True),
    )
    stream = resid_full.astype(jnp.float32) + total
    stream_sq = jnp.mean(stream * stream, axis=-1, keepdims=True)
    moe_in = (stream * lax.rsqrt(stream_sq + EPSILON) * gain_full.astype(jnp.float32)).astype(
        jnp.bfloat16
    )
    stream_mine = lax.dynamic_slice_in_dim(stream, lax.axis_index("head") * width, width, 1)
    experts = router.shape[1]
    capacity = 3 * rows * TOP // (2 * experts)
    logits = jnp.dot(moe_in, router, preferred_element_type=jnp.float32)
    picked_mask = expert_ids[:, :, None] == jnp.arange(experts, dtype=jnp.int32)[None, None, :]
    picked = jnp.sum(jnp.where(picked_mask, logits[:, None, :], 0.0), axis=-1)
    mix_weights = jax.nn.sigmoid(picked - picked[:, ::-1])
    flat_ids = expert_ids.reshape(-1)
    onehot = (flat_ids[:, None] == jnp.arange(experts, dtype=jnp.int32)[None, :]).astype(jnp.int32)
    before = jnp.cumsum(onehot, axis=0) - onehot
    position = jnp.sum(before * onehot, axis=1)
    slot = flat_ids * capacity + position
    owner = jnp.arange(rows * TOP, dtype=jnp.int32) // TOP
    slot_token = jnp.zeros((experts * capacity,), jnp.int32).at[slot].set(owner)
    filled = jnp.zeros((experts * capacity,), jnp.bool_).at[slot].set(True)
    blank = jnp.zeros((), jnp.bfloat16)
    outgoing = jnp.where(filled[:, None], moe_in[slot_token], blank).reshape(
        experts, capacity, full
    )
    arriving = lax.all_to_all(outgoing, "ctx", split_axis=0, concat_axis=0, tiled=True)
    flat = arriving.reshape(-1, full)
    gate = jnp.dot(flat, gate_weight[0], preferred_element_type=jnp.float32)
    up = jnp.dot(flat, up_weight[0], preferred_element_type=jnp.float32)
    activated = (jax.nn.silu(gate) * up).astype(jnp.bfloat16)
    partial_value = jnp.dot(activated, down_weight[0], preferred_element_type=jnp.float32).reshape(
        arriving.shape[0], arriving.shape[1], full
    )
    summed = lax.psum_scatter(
        partial_value.astype(jnp.bfloat16), "head", scatter_dimension=2, tiled=True
    )
    returned = lax.all_to_all(summed, "ctx", split_axis=0, concat_axis=0, tiled=True)
    picked_rows = returned.reshape(experts * capacity, width)[slot].astype(jnp.float32)
    moe_out = jnp.sum(picked_rows.reshape(rows, TOP, width) * mix_weights[:, :, None], axis=1)
    return stream_mine + moe_out


def solution(mesh):
    placed = (
        P("ctx", "head"),
        P("ctx", "head"),
        P("ctx", "head"),
        P("ctx", "head"),
        P("head"),
        P("ctx", "head"),
        P("ctx", "head"),
        P("head"),
        P(),
        P("ctx", None),
        P("ctx", None, "head"),
        P("ctx", None, "head"),
        P("ctx", "head", None),
    )
    return jax.shard_map(
        on_device, mesh=mesh, in_specs=placed, out_specs=P("ctx", "head"), check_vma=False
    )
```

profile of v0, /device:TPU:1, one launch (start us, length us, event | category | flops | bytes accessed | tf_op | source)
XLA Modules:
  0.0 506.1 jit_solution(9988113426470211069)
XLA Ops:
  14.7 23.1 %all-gather.1 = f32[32,1,4]{2,1,0:T(1,128)S(1)} all-gather(f32[1,1,4]{2,1,0:T(1,128)S(1)} %bitcast.144), channel_id=1, replica_groups=mesh['ctx'=32,'head'=8] {'ctx'}, dimensions={0}, use_global_device_ids=true | all-gather | bytes 528 | tf_op jit(solution)/shard_map/all_gather | solution.py:16
  37.8 36.7 %all-gather.11.cloned.1.call-done = f32[128,128,128]{2,1,0:T(8,128)} async-done(((f32[4,128,128]{2,1,0:T(8,128)}), f32[128,128,128]{2,1,0:T(8,128)}) %all-gather.11.cloned.1.call-update) | async-done | bytes 8388624 | tf_op jit(solution)/shard_map/all_gather | solution.py:16
  74.5 34.0 %while.14 = (s32[]{:T(128)}, f32[4,128,128]{2,1,0:T(8,128)S(1)}, s32[]{:T(128)}, f32[32,4]{1,0:T(8,128)S(1)}, f32[32,4,128,128]{3,2,1,0:T(8,128)}, /*index=5*/s32[]{:T(128)}, s32[]{:T(128)}) while((s32[]{:T(128)}, f32[4,128,128]{2,1,0:T(8,128)S(1)}, s32[]{:T(128)}, f32[32,4]{1,0:T(8,128)S(1)}, f32[32,4,128,128]{3,2,1,0:T(8,128)}, ...), condition=%wide.region_3.4_spmd.clone, body=%wide.region_2.3_spmd.clone.sunk | while | flops 262148 | bytes 786593 | solution.py:25
  110.2 16.4 %all-gather.9.cloned.1.call-done = bf16[3072,512]{1,0:T(8,128)(2,1)} async-done(((bf16[96,512]{1,0:T(8,128)(2,1)}), bf16[3072,512]{1,0:T(8,128)(2,1)}) %all-gather.9.cloned.1.call-update) | async-done | bytes 3145744 | tf_op jit(solution)/shard_map/all_gather | solution.py:80
  126.6 4.6 fusion.51
  132.4 19.9 %all-gather.2 = bf16[8,1,384]{2,1,0:T(2,128)(2,1)S(1)} all-gather(bf16[1,1,384]{2,1,0:T(2,128)(2,1)S(1)} %reshape.192), channel_id=1, replica_groups=mesh['ctx'=32,'head'=8] {'head'}, dimensions={0}, use_global_device_ids=true | all-gather | bytes 6912 | tf_op jit(solution)/shard_map/all_gather | solution.py:89
  154.1 2.4 scatter_custom_fusion.1
  156.6 2.4 scatter_custom_fusion
  159.2 3.0 all-gather.7.cloned.1.call-done
  162.1 96.9 %all-reduce.2.cloned.1.call-done = f32[256,3072]{1,0:T(8,128)} async-done(((f32[256,3072]{1,0:T(8,128)}), f32[256,3072]{1,0:T(8,128)}) %all-reduce.2.cloned.1.call-update) | async-done | bytes 3145744 | tf_op jit(solution)/shard_map/psum | solution.py:86
  259.0 2.8 multiply_reduce_fusion
  264.0 5.0 gather_fusion
  268.9 2.7 broadcast_select_fusion
  271.7 64.4 %all_to_all.10 = bf16[32,24,3072]{2,1,0:T(8,128)(2,1)S(1)} all-to-all(bf16[32,24,3072]{2,1,0:T(8,128)(2,1)S(1)} %broadcast_select_fusion), channel_id=1, replica_groups=mesh['ctx'=32,'head'=8] {'ctx'}, dimensions={0} | all-to-all | bytes 9437184 | tf_op jit(solution)/shard_map/all_to_all | solution.py:115
  336.0 3.8 fusion.4
  339.9 3.9 multiply_convert_fusion.1
  343.8 5.5 %convolution_convert_fusion = bf16[32,24,3072]{2,1,0:T(8,128)(2,1)} fusion(bf16[32,24,640]{2,1,0:T(8,128)(2,1)S(1)} %bitcast.145, bf16[1,640,3072]{2,1,0:T(8,128)(2,1)S(1)} %copy-done.9), kind=kOutput, calls=%fused_computation.7 | convolution fusion | flops 3022258176 | bytes 9633792 | tf_op jit(solution)/shard_map/dot_general | solution.py:120
  349.3 22.6 %copy.119 = bf16[32,24,3072]{1,0,2:T(8,128)(2,1)} copy(bf16[32,24,3072]{2,1,0:T(8,128)(2,1)} %convolution_convert_fusion) | data formatting | bytes 9437184
  371.9 35.3 %reshape.196 = bf16[3072,768]{1,0:T(8,128)(2,1)} reshape(bf16[3072,32,24]{2,1,0:T(8,128)(2,1)} %bitcast.124) | data formatting | bytes 9437184
  407.3 55.4 %reduce-scatter.4.cloned.1.call-done = bf16[384,768]{1,0:T(8,128)(2,1)} async-done(((bf16[3072,768]{1,0:T(8,128)(2,1)}), bf16[384,768]{1,0:T(8,128)(2,1)}) %reduce-scatter.4.cloned.1.call-update) | async-done | bytes 589840
  462.7 6.8 %reshape.197 = bf16[384,32,24]{2,1,0:T(8,128)(2,1)} reshape(bf16[384,768]{1,0:T(8,128)(2,1)} %reduce-scatter.4.cloned.1.call-done) | data formatting | bytes 1179648
  469.5 5.2 %copy.120 = bf16[32,24,384]{2,1,0:T(8,128)(2,1)} copy(bf16[32,24,384]{1,0,2:T(8,128)(2,1)} %bitcast.127) | data formatting | bytes 1179648
  474.7 7.6 %all-to-all-start.1 = ((bf16[32,24,384]{2,1,0:T(8,128)(2,1)}), bf16[32,24,384]{2,1,0:T(8,128)(2,1)S(1)}, u32[]{:S(2)}, u32[]{:S(2)}) async-start(bf16[32,24,384]{2,1,0:T(8,128)(2,1)} %copy.120), calls=%async_computation.1 | async-start | bytes 1179648 | tf_op jit(solution)/shard_map/all_to_all | solution.py:126
  483.2 11.3 %all-to-all-done.1 = bf16[32,24,384]{2,1,0:T(8,128)(2,1)S(1)} async-done(((bf16[32,24,384]{2,1,0:T(8,128)(2,1)}), bf16[32,24,384]{2,1,0:T(8,128)(2,1)S(1)}, u32[]{:S(2)}, u32[]{:S(2)}) %all-to-all-start.1) | async-done | bytes 589856 | tf_op jit(solution)/shard_map/all_to_all | solution.py:126
  (144 shorter events, 53.8 us)
Async XLA Ops:
  6.5 102.0 %copy-start = (bf16[256,512]{1,0:T(8,128)(2,1)S(1)}, bf16[256,512]{1,0:T(8,128)(2,1)}, u32[]{:S(2)}) copy-start(bf16[256,512]{1,0:T(8,128)(2,1)} %param.15) | copy-start | bytes 786436
  6.5 68.0 %all-gather.11.cloned.1.call-start = ((), (), s32[]{:S(2)}) async-start(), calls=%async_computation.6 | async-start | bytes 8650752 | tf_op jit(solution)/shard_map/all_gather | solution.py:16
  10.3 99.1 %copy-start.3 = (bf16[256,512]{1,0:T(8,128)(2,1)S(1)}, bf16[256,512]{1,0:T(8,128)(2,1)}, u32[]{:S(2)}) copy-start(bf16[256,512]{1,0:T(8,128)(2,1)} %param.17) | copy-start | bytes 786436
  12.4 114.2 %all-gather.9.cloned.1.call-start = ((), (), s32[]{:S(2)}) async-start(), calls=%async_computation.4 | async-start | bytes 3244032 | tf_op jit(solution)/shard_map/all_gather | solution.py:80
  13.2 149.0 %all-gather.7.cloned.1.call-start = ((), (), s32[]{:S(2)}) async-start(), calls=%async_computation.3 | async-start | bytes 1769472 | tf_op jit(solution)/shard_map/all_gather | solution.py:88
  13.9 245.1 %all-reduce.2.cloned.1.call-start = ((), (), s32[]{:S(2)}) async-start(), calls=%async_computation.5 | async-start | bytes 6291456 | tf_op jit(solution)/shard_map/psum | solution.py:86
  131.2 0.7 copy-start.5
  131.2 1.1 copy-start.6
  131.2 331.4 %reduce-scatter.4.cloned.1.call-start = ((), (), s32[]{:S(2)}) async-start(), calls=%async_computation.7 | async-start | bytes 5308416
  261.8 1.6 copy-start.2
  271.6 64.4 %copy-start.7 = (bf16[1,3072,640]{2,1,0:T(8,128)(2,1)S(1)}, bf16[1,3072,640]{2,1,0:T(8,128)(2,1)}, u32[]{:S(2)}) copy-start(bf16[1,3072,640]{2,1,0:T(8,128)(2,1)} %param.25) | copy-start | bytes 11796484
  336.0 3.8 copy-start.8
  339.9 3.9 copy-start.9
  469.5 12.8 %copy-start.4 = (bf16[3072,32]{0,1:T(8,128)(2,1)S(1)}, bf16[3072,32]{0,1:T(8,128)(2,1)}, u32[]{:S(2)}) copy-start(bf16[3072,32]{0,1:T(8,128)(2,1)} %param.23) | copy-start | bytes 589828
  474.7 19.7 %all-to-all-start.1 = ((bf16[32,24,384]{2,1,0:T(8,128)(2,1)}), bf16[32,24,384]{2,1,0:T(8,128)(2,1)S(1)}, u32[]{:S(2)}, u32[]{:S(2)}) async-start(bf16[32,24,384]{2,1,0:T(8,128)(2,1)} %copy.120), calls=%async_computation.1 | async-start | bytes 1179648 | tf_op jit(solution)/shard_map/all_to_all | solution.py:126
  494.4 5.1 %copy-start.1 = (bf16[256,512]{1,0:T(8,128)(2,1)S(1)}, bf16[256,512]{1,0:T(8,128)(2,1)}, u32[]{:S(2)}) copy-start(bf16[256,512]{1,0:T(8,128)(2,1)} %param.15) | copy-start | bytes 786436
Sparse Core Ops, SparseCore 0:
  12.5 61.9 all-gather.10
  77.1 49.4 all-gather.8
  128.4 33.6 all-gather.6
  164.4 94.6 all-reduce.1
  407.4 55.2 reduce-scatter.3
where the time goes:
time: 509 us; the launch traced here: 506 us
  waiting for transfers between devices  221 us (43%)
  blocking collectives  107 us (21%)
  local copies, waits for them, and re-layouts  88 us (17%)
  other arithmetic  45.4 us (9%)
  matrix products  21.9 us (4%)
  between operations  13.5 us (3%)
  starting transfers between devices  7.74 us (2%)
    psum x1, waiting for transfers between devices, on_device(): total = lax.psum(partial_proj, 'head')  96.9 us
    unnamed x27, local copies, waits for them, and re-layouts  72.4 us
    all_to_all x1, blocking collectives, on_device(): lax.all_to_all(outgoing, 'ctx', split_axis=0, concat_axis=0, tiled=True)  64.4 us
    unnamed x6, waiting for transfers between devices  56.8 us
    all_gather x1, waiting for transfers between devices, entering(): pieces = jax.tree.map(lambda part: lax.all_gather(part, axis), value)  36.7 us
    select_n x31, other arithmetic, turn(): jnp.where(position < mine, new, old)  32.8 us
    all_gather x1, blocking collectives, entering(): pieces = jax.tree.map(lambda part: lax.all_gather(part, axis), value)  23.1 us
    all_gather x1, blocking collectives, on_device(): lax.all_gather(norm_gain, 'head', axis=0, tiled=True)  19.9 us
  transfers between devices with their start and end apart: 6, of which 6 were waited for; matrix products, arithmetic and copies ran while one was open for 9% of the time, Pallas kernels for 0%

commit v1 on v0

--- a/solution.py
+++ b/solution.py
@@ -11,24 +11,31 @@
 EPSILON = 1e-05
 
 
-def entering(value, axis, join, neutral):
-    count, mine = (lax.axis_size(axis), lax.axis_index(axis))
-    pieces = jax.tree.map(lambda part: lax.all_gather(part, axis), value)
-    total = jax.tree.map(
-        lambda part, zero: jnp.full_like(part, 0) + jnp.asarray(zero, part.dtype), value, neutral
-    )
-
-    def turn(position, total):
-        longer = join(total, jax.tree.map(lambda part: part[position], pieces))
-        return jax.tree.map(lambda new, old: jnp.where(position < mine, new, old), longer, total)
-
-    return lax.fori_loop(0, count - 1, turn, total)
+def combine(earlier, later):
+    rows = HEAD_DIM
+    decay_late = later[:, rows:rows + 1, 0:1]
+    state = decay_late * earlier[:, :rows] + later[:, :rows]
+    decay = earlier[:, rows:rows + 1] * later[:, rows:rows + 1]
+    pad = jnp.zeros((later.shape[0], later.shape[1] - rows - 1, later.shape[2]), later.dtype)
+    return jnp.concatenate([state, decay, pad], axis=1)
 
 
-def chain_states(earlier, later):
-    decay_early, state_early = earlier
-    decay_late, state_late = later
-    return (decay_early * decay_late, decay_late[:, None, None] * state_early + state_late)
+def exclusive_scan(packed, axis):
+    count, mine = lax.axis_size(axis), lax.axis_index(axis)
+    rows = HEAD_DIM
+    identity = jnp.zeros_like(packed).at[:, rows].set(1.0)
+    window = packed
+    before = identity
+    shift = 1
+    while shift < count:
+        pairs = [(j, j + shift) for j in range(count - shift)]
+        got = lax.ppermute(window, axis, pairs)
+        got = jnp.where(mine >= shift, got, identity)
+        before = combine(got, before)
+        if 2 * shift < count:
+            window = combine(got, window)
+        shift *= 2
+    return before[:, :rows]
 
 
 def on_device(
@@ -48,6 +55,7 @@
 ):
     rows = queries.shape[0]
     heads_here = log_decay.shape[1]
+    groups = lax.axis_size("head")
     query_heads = queries.reshape(rows, heads_here, HEAD_DIM)
     key_heads = key_rows.reshape(rows, heads_here, HEAD_DIM)
     value_heads = values.reshape(rows, heads_here, HEAD_DIM)
@@ -63,8 +71,10 @@
     keys_tail = key_heads.astype(jnp.float32) * tail[:, :, None]
     local_state = jnp.einsum("jhd,jhe->hde", keys_tail, value_wide, precision=HIGH)
     shard_decay = jnp.exp(-cumulative[-1])
-    identity = (jnp.ones_like(shard_decay), jnp.zeros_like(local_state))
-    incoming = entering((shard_decay, local_state), "ctx", chain_states, identity)[1]
+    decay_rows = jnp.broadcast_to(shard_decay[:, None, None], (heads_here, 1, HEAD_DIM))
+    pad = jnp.zeros((heads_here, 7, HEAD_DIM), jnp.float32)
+    packed = jnp.concatenate([local_state, decay_rows, pad], axis=1)
+    incoming = exclusive_scan(packed, "ctx")
     query_decayed = query_heads.astype(jnp.float32) * jnp.exp(-cumulative)[:, :, None]
     outer = jnp.einsum("thd,hde->the", query_decayed, incoming, precision=HIGH)
     mixed = inner + outer
@@ -75,25 +85,30 @@
         .astype(jnp.bfloat16)
         .reshape(rows, heads_here * HEAD_DIM)
     )
-    partial_proj = lax.dot_general(
-        normed,
-        lax.all_gather(out_weight, "ctx", axis=0, tiled=True),
-        (((1,), (1,)), ((), ())),
-        preferred_element_type=jnp.float32,
+    width = residual.shape[1]
+    full = width * groups
+    weight_all = lax.all_gather(out_weight, "ctx", axis=0, tiled=True).reshape(
+        groups, width, heads_here * HEAD_DIM
     )
-    width = residual.shape[1]
-    full = width * lax.axis_size("head")
-    total = lax.psum(partial_proj, "head")
-    resid_full, gain_full = (
-        lax.all_gather(residual, "head", axis=1, tiled=True),
-        lax.all_gather(norm_gain, "head", axis=0, tiled=True),
-    )
-    stream = resid_full.astype(jnp.float32) + total
-    stream_sq = jnp.mean(stream * stream, axis=-1, keepdims=True)
-    moe_in = (stream * lax.rsqrt(stream_sq + EPSILON) * gain_full.astype(jnp.float32)).astype(
-        jnp.bfloat16
-    )
-    stream_mine = lax.dynamic_slice_in_dim(stream, lax.axis_index("head") * width, width, 1)
+    partial_proj = jnp.einsum(
+        "tk,gck->gtc", normed, weight_all, preferred_element_type=jnp.float32
+    ).astype(jnp.bfloat16)
+    pieces = lax.all_to_all(partial_proj, "head", 0, 0, tiled=True)
+    stream_mine = residual.astype(jnp.float32) + jnp.sum(pieces.astype(jnp.float32), axis=0)
+    sq_part = jnp.sum(stream_mine * stream_mine, axis=1)
+    sq_hi = sq_part.astype(jnp.bfloat16)
+    sq_lo = (sq_part - sq_hi.astype(jnp.float32)).astype(jnp.bfloat16)
+    extra = jnp.zeros((8, width), jnp.bfloat16)
+    extra = extra.at[0].set(norm_gain)
+    extra = extra.at[1, :rows].set(sq_hi)
+    extra = extra.at[2, :rows].set(sq_lo)
+    payload = jnp.concatenate([stream_mine.astype(jnp.bfloat16), extra], axis=0)
+    gathered = lax.all_gather(payload, "head", axis=1, tiled=True)
+    stream_wide = gathered[:rows].astype(jnp.float32)
+    gain_full = gathered[rows].astype(jnp.float32)
+    sq_parts = gathered[rows + 1 : rows + 3].astype(jnp.float32).reshape(2, groups, width)
+    stream_sq = jnp.sum(sq_parts[:, :, :rows], axis=(0, 1))[:, None] / full
+    moe_in = (stream_wide * lax.rsqrt(stream_sq + EPSILON) * gain_full).astype(jnp.bfloat16)
     experts = router.shape[1]
     capacity = 3 * rows * TOP // (2 * experts)
     logits = jnp.dot(moe_in, router, preferred_element_type=jnp.float32)
@@ -117,12 +132,12 @@
     gate = jnp.dot(flat, gate_weight[0], preferred_element_type=jnp.float32)
     up = jnp.dot(flat, up_weight[0], preferred_element_type=jnp.float32)
     activated = (jax.nn.silu(gate) * up).astype(jnp.bfloat16)
-    partial_value = jnp.dot(activated, down_weight[0], preferred_element_type=jnp.float32).reshape(
-        arriving.shape[0], arriving.shape[1], full
-    )
-    summed = lax.psum_scatter(
-        partial_value.astype(jnp.bfloat16), "head", scatter_dimension=2, tiled=True
-    )
+    down = down_weight[0].reshape(down_weight.shape[1], groups, width)
+    partial_value = jnp.einsum(
+        "rf,fgc->grc", activated, down, preferred_element_type=jnp.float32
+    ).astype(jnp.bfloat16)
+    summed = lax.psum_scatter(partial_value, "head", scatter_dimension=0, tiled=True)
+    summed = summed.reshape(arriving.shape[0], arriving.shape[1], width)
     returned = lax.all_to_all(summed, "ctx", split_axis=0, concat_axis=0, tiled=True)
     picked_rows = returned.reshape(experts * capacity, width)[slot].astype(jnp.float32)
     moe_out = jnp.sum(picked_rows.reshape(rows, TOP, width) * mix_weights[:, :, None], axis=1)

time: 509 us -> 346 us (0.68)
  blocking collectives: 107 us -> 0 us
  local copies, waits for them, and re-layouts: 88 us -> 22.9 us
  starting transfers between devices: 7.74 us -> 51.5 us
  other arithmetic: 45.4 us -> 14.6 us
    psum x1 -> x0, waiting for transfers between devices: 96.9 us -> none  [on_device(): total = lax.psum(partial_proj, 'head')]
    all_to_all x0 -> x2, waiting for transfers between devices: none -> 91.3 us  [the longest x1 51 us: on_device(): lax.all_to_all(outgoing, 'ctx', split_axis=0, concat_axis=0, tiled=True)]
    unnamed x27 -> x24, local copies, waits for them, and re-layouts: 72.4 us -> 5.21 us
    all_to_all x1 -> x0, blocking collectives: 64.4 us -> none  [on_device(): lax.all_to_all(outgoing, 'ctx', split_axis=0, concat_axis=0, tiled=True)]
    reduce_scatter x0 -> x1, waiting for transfers between devices: none -> 57.3 us  [on_device(): lax.psum_scatter(partial_value, 'head', scatter_dimension=0, tiled=True)]
    unnamed x6 -> x3, waiting for transfers between devices: 56.8 us -> 0.05 us
    all_gather x2 -> x0, blocking collectives: 43 us -> none  [the longest x1 23.1 us: entering(): pieces = jax.tree.map(lambda part: lax.all_gather(part, axis), value)]
    select_n x31 -> x4, other arithmetic: 32.8 us -> 0.12 us  [exclusive_scan(): got = jnp.where(mine >= shift, got, identity)]
  transfers between devices with their start and end apart: 6 -> 11, of which waited for: 6 -> 11; matrix products, arithmetic and copies ran while one was open for 9% -> 5% of each run, Pallas kernels for 0% -> 0%
where the time goes in v1:
time: 346 us; the launch traced here: 345 us
  waiting for transfers between devices  216 us (62%)
  starting transfers between devices  51.5 us (15%)
  matrix products  26.3 us (8%)
  local copies, waits for them, and re-layouts  22.9 us (7%)
  other arithmetic  14.6 us (4%)
  between operations  13.7 us (4%)
    reduce_scatter x1, waiting for transfers between devices, on_device(): lax.psum_scatter(partial_value, 'head', scatter_dimension=0, tiled=True)  57.3 us
    all_to_all x1, waiting for transfers between devices, on_device(): lax.all_to_all(outgoing, 'ctx', split_axis=0, concat_axis=0, tiled=True)  51 us
    all_to_all x1, waiting for transfers between devices, on_device(): pieces = lax.all_to_all(partial_proj, 'head', 0, 0, tiled=True)  40.3 us
    ppermute x5, starting transfers between devices, exclusive_scan(): got = lax.ppermute(window, axis, pairs)  24.1 us
    all_gather x1, waiting for transfers between devices, on_device(): gathered = lax.all_gather(payload, 'head', axis=1, tiled=True)  22.7 us
    ppermute x5, waiting for transfers between devices, exclusive_scan(): got = lax.ppermute(window, axis, pairs)  18.1 us
    all_gather x1, waiting for transfers between devices, on_device(): lax.all_gather(out_weight, 'ctx', axis=0, tiled=True)  15.2 us
    all_to_all x1, starting transfers between devices, on_device(): lax.all_to_all(outgoing, 'ctx', split_axis=0, concat_axis=0, tiled=True)  12.7 us
  transfers between devices with their start and end apart: 11, of which 11 were waited for; matrix products, arithmetic and copies ran while one was open for 5% of the time, Pallas kernels for 0%

profile of v1, /device:TPU:1, one launch (start us, length us, event | category | flops | bytes accessed | tf_op | source)
XLA Modules:
  0.0 345.0 jit_solution(16803198207321830222)
XLA Ops:
  11.9 4.5 %collective-permute-start = (f32[4,136,128]{2,1,0:T(8,128)S(1)}, f32[4,136,128]{2,1,0:T(8,128)S(1)}, u32[]{:S(2)}, u32[]{:S(2)}) collective-permute-start(f32[4,136,128]{2,1,0:T(8,128)S(1)} %maximum_maximum_fusion), channel_id=1, source_target_pairs={{0,8},{8,16},{16,24},{24,32},{32,40},{40,48},{48,56},{56,64},{64,7... | collective-permute-start | bytes 835592 | tf_op jit(solution)/shard_map/ppermute | solution.py:32
  16.5 3.4 collective-permute-done
  23.5 4.4 %collective-permute-done.1 = f32[4,136,128]{2,1,0:T(8,128)S(1)} collective-permute-done((f32[4,136,128]{2,1,0:T(8,128)S(1)}, f32[4,136,128]{2,1,0:T(8,128)S(1)}, u32[]{:S(2)}, u32[]{:S(2)}) %collective-permute-start.1) | collective-permute-done | bytes 278560 | tf_op jit(solution)/shard_map/ppermute | solution.py:32
  28.2 5.1 %collective-permute-start.2 = (f32[4,136,128]{2,1,0:T(8,128)S(1)}, f32[4,136,128]{2,1,0:T(8,128)S(1)}, u32[]{:S(2)}, u32[]{:S(2)}) collective-permute-start(f32[4,136,128]{2,1,0:T(8,128)S(1)} %maximum_maximum_fusion.2), channel_id=1, source_target_pairs={{0,32},{8,40},{16,48},{24,56},{32,64},{40,72},{48,80},{56,88},{64,... | collective-permute-start | bytes 835592 | tf_op jit(solution)/shard_map/ppermute | solution.py:32
  34.1 3.2 collective-permute-done.2
  37.5 5.9 %collective-permute-start.3 = (f32[4,136,128]{2,1,0:T(8,128)S(1)}, f32[4,136,128]{2,1,0:T(8,128)S(1)}, u32[]{:S(2)}, u32[]{:S(2)}) collective-permute-start(f32[4,136,128]{2,1,0:T(8,128)S(1)} %maximum_maximum_fusion.3), channel_id=1, source_target_pairs={{0,64},{8,72},{16,80},{24,88},{32,96},{40,104},{48,112},{56,120},{... | collective-permute-start | bytes 835592 | tf_op jit(solution)/shard_map/ppermute | solution.py:32
  43.6 3.9 %collective-permute-done.3 = f32[4,136,128]{2,1,0:T(8,128)S(1)} collective-permute-done((f32[4,136,128]{2,1,0:T(8,128)S(1)}, f32[4,136,128]{2,1,0:T(8,128)S(1)}, u32[]{:S(2)}, u32[]{:S(2)}) %collective-permute-start.3) | collective-permute-done | bytes 278560 | tf_op jit(solution)/shard_map/ppermute | solution.py:32
  47.7 5.4 %collective-permute-start.4 = (f32[4,136,128]{2,1,0:T(8,128)S(1)}, f32[4,136,128]{2,1,0:T(8,128)S(1)}, u32[]{:S(2)}, u32[]{:S(2)}) collective-permute-start(f32[4,136,128]{2,1,0:T(8,128)S(1)} %maximum_maximum_fusion.4), channel_id=1, source_target_pairs={{0,128},{8,136},{16,144},{24,152},{32,160},{40,168},{48,176},{56,1... | collective-permute-start | bytes 835592 | tf_op jit(solution)/shard_map/ppermute | solution.py:32
  57.6 15.2 %all-gather.3.cloned.1.call-done = bf16[3072,512]{1,0:T(8,128)(2,1)} async-done(((bf16[96,512]{1,0:T(8,128)(2,1)}), bf16[3072,512]{1,0:T(8,128)(2,1)}) %all-gather.3.cloned.1.call-update) | async-done | bytes 3145744 | tf_op jit(solution)/shard_map/all_gather | solution.py:90
  72.8 4.1 %fusion.10 = bf16[8,256,384]{2,1,0:T(8,128)(2,1)} fusion(bf16[256,512,1]{0,1,2:T(8,128)(2,1)S(1)} %bitcast.127, bf16[8,384,512]{2,1,0:T(8,128)(2,1)} %bitcast.126), kind=kOutput, calls=%fused_computation.16 | convolution fusion | flops 806092800 | bytes 4980736 | tf_op jit(solution)/shard_map/tk,gck->gtc/dot_general | solution.py:93
  76.9 7.1 %all-to-all-start = ((bf16[8,256,384]{2,1,0:T(8,128)(2,1)}), bf16[8,256,384]{2,1,0:T(8,128)(2,1)S(1)}, u32[]{:S(2)}, u32[]{:S(2)}) async-start(bf16[8,256,384]{2,1,0:T(8,128)(2,1)} %fusion.10), calls=%async_computation | async-start | bytes 3145728 | tf_op jit(solution)/shard_map/all_to_all | solution.py:96
  84.1 40.3 %all-to-all-done = bf16[8,256,384]{2,1,0:T(8,128)(2,1)S(1)} async-done(((bf16[8,256,384]{2,1,0:T(8,128)(2,1)}), bf16[8,256,384]{2,1,0:T(8,128)(2,1)S(1)}, u32[]{:S(2)}, u32[]{:S(2)}) %all-to-all-start) | async-done | bytes 1572896 | tf_op jit(solution)/shard_map/all_to_all | solution.py:96
  133.3 22.7 %all-gather.5.cloned.1.call-done = bf16[264,3072]{1,0:T(8,128)(2,1)} async-done(((bf16[264,384]{1,0:T(8,128)(2,1)}), bf16[264,3072]{1,0:T(8,128)(2,1)}) %all-gather.5.cloned.1.call-update) | async-done | bytes 1622032 | tf_op jit(solution)/shard_map/all_gather | solution.py:106
  159.6 5.1 %gather_fusion = bf16[768,3072]{1,0:T(8,128)(2,1)} fusion(bf16[256,3072]{1,0:T(8,128)(2,1)S(1)} %multiply_convert_fusion, s32[1024]{0:T(1024)S(1)} %pad_clamp_fusion.1), kind=kCustom, calls=%fused_computation | custom fusion | bytes 9440256 | tf_op jit(solution)/shard_map/gather | solution.py:127
  164.7 4.8 %broadcast_select_fusion = bf16[32,24,3072]{2,1,0:T(8,128)(2,1)} fusion(bf16[32,24,3072]{2,1,0:T(8,128)(2,1)} %bitcast.123, pred[32,24]{1,0:T(8,128)(4,1)S(1)} %broadcast_in_dim.87), kind=kLoop, calls=%fused_computation.5 | loop fusion | flops 2359296 | bytes 9437952 | tf_op jit(solution)/shard_map/jit(_where)/select_n | solution.py:127
  169.5 12.7 %all-to-all-start.1 = ((bf16[32,24,3072]{2,1,0:T(8,128)(2,1)}), bf16[32,24,3072]{2,1,0:T(8,128)(2,1)}, u32[]{:S(2)}, u32[]{:S(2)}) async-start(bf16[32,24,3072]{2,1,0:T(8,128)(2,1)} %broadcast_select_fusion), calls=%async_computation.1 | async-start | bytes 9437184 | tf_op jit(solution)/shard_map/all_to_all | solution.py:130
  182.3 5.0 %copy.106 = bf16[80,8,8,384]{3,2,1,0:T(8,128)(2,1)} copy(bf16[80,8,8,384]{3,1,2,0:T(8,128)(2,1)} %bitcast.124) | data formatting | bytes 7864320
  187.3 51.0 %all-to-all-done.1 = bf16[32,24,3072]{2,1,0:T(8,128)(2,1)} async-done(((bf16[32,24,3072]{2,1,0:T(8,128)(2,1)}), bf16[32,24,3072]{2,1,0:T(8,128)(2,1)}, u32[]{:S(2)}, u32[]{:S(2)}) %all-to-all-start.1) | async-done | bytes 4718624 | tf_op jit(solution)/shard_map/all_to_all | solution.py:130
  238.3 7.0 %fusion.2 = f32[768,640]{1,0:T(8,128)S(1)} fusion(bf16[768,3072]{1,0:T(8,128)(2,1)} %bitcast.16, bf16[1,3072,640]{2,1,0:T(8,128)(2,1)} %param.31), kind=kOutput, calls=%fused_computation.8 | convolution fusion | flops 3019898880 | bytes 10616832 | tf_op jit(solution)/shard_map/dot_general | solution.py:132
  245.3 6.4 %fusion.11 = bf16[768,640,1]{1,0,2:T(8,128)(2,1)S(1)} fusion(bf16[768,3072]{1,0:T(8,128)(2,1)} %bitcast.16, bf16[1,3072,640]{2,1,0:T(8,128)(2,1)S(1)} %copy-done.9, f32[768,640]{1,0:T(8,128)S(1)} %fusion.2), kind=kOutput, calls=%fused_computation.18 | convolution fusion | flops 3022848000 | bytes 11599872 | tf_op jit(solution)/shard_map/dot_general | solution.py:133
  251.7 5.5 %convert_bitcast_fusion = bf16[8,768,384]{2,1,0:T(8,128)(2,1)} fusion(bf16[768,640,1]{1,0,2:T(8,128)(2,1)S(1)} %fusion.11, bf16[640,8,384]{2,1,0:T(8,128)(2,1)S(1)} %bitcast.125), kind=kOutput, calls=%fused_computation.4 | convolution fusion | flops 3022258176 | bytes 9633792 | tf_op jit(solution)/shard_map/rf,fgc->grc/dot_general | solution.py:136
  257.3 57.3 %reduce-scatter.2.cloned.1.call-done = bf16[1,768,384]{2,1,0:T(8,128)(2,1)} async-done(((bf16[8,768,384]{2,1,0:T(8,128)(2,1)}), bf16[1,768,384]{2,1,0:T(8,128)(2,1)}) %reduce-scatter.2.cloned.1.call-update) | async-done | bytes 589840 | tf_op jit(solution)/shard_map/reduce_scatter | solution.py:139
  314.6 7.6 %all-to-all-start.2 = ((bf16[32,24,384]{2,1,0:T(8,128)(2,1)}), bf16[32,24,384]{2,1,0:T(8,128)(2,1)S(1)}, u32[]{:S(2)}, u32[]{:S(2)}) async-start(bf16[32,24,384]{2,1,0:T(8,128)(2,1)} %bitcast.130), calls=%async_computation.3 | async-start | bytes 1179648 | tf_op jit(solution)/shard_map/all_to_all | solution.py:141
  323.0 11.3 %all-to-all-done.2 = bf16[32,24,384]{2,1,0:T(8,128)(2,1)S(1)} async-done(((bf16[32,24,384]{2,1,0:T(8,128)(2,1)}), bf16[32,24,384]{2,1,0:T(8,128)(2,1)S(1)}, u32[]{:S(2)}, u32[]{:S(2)}) %all-to-all-start.2) | async-done | bytes 589856 | tf_op jit(solution)/shard_map/all_to_all | solution.py:141
  (119 shorter events, 32.3 us)
Async XLA Ops:
  6.5 26.8 %copy-start = (bf16[256,512]{1,0:T(8,128)(2,1)S(1)}, bf16[256,512]{1,0:T(8,128)(2,1)}, u32[]{:S(2)}) copy-start(bf16[256,512]{1,0:T(8,128)(2,1)} %param.21) | copy-start | bytes 786436
  6.5 21.4 %copy-start.1 = (f32[4,136,128]{2,1,0:T(8,128)S(1)}, f32[4,136,128]{2,1,0:T(8,128)}, u32[]{:S(2)}) copy-start(f32[4,136,128]{2,1,0:T(8,128)} %constant.172.clone.1) | copy-start | bytes 835588
  6.5 66.2 %all-gather.3.cloned.1.call-start = ((), (), s32[]{:S(2)}) async-start(), calls=%async_computation.4 | async-start | bytes 3244032 | tf_op jit(solution)/shard_map/all_gather | solution.py:90
  9.2 24.2 %copy-start.4 = (bf16[256,512]{1,0:T(8,128)(2,1)S(1)}, bf16[256,512]{1,0:T(8,128)(2,1)}, u32[]{:S(2)}) copy-start(bf16[256,512]{1,0:T(8,128)(2,1)} %param.23) | copy-start | bytes 786436
  11.9 8.0 %collective-permute-start = (f32[4,136,128]{2,1,0:T(8,128)S(1)}, f32[4,136,128]{2,1,0:T(8,128)S(1)}, u32[]{:S(2)}, u32[]{:S(2)}) collective-permute-start(f32[4,136,128]{2,1,0:T(8,128)S(1)} %maximum_maximum_fusion), channel_id=1, source_target_pairs={{0,8},{8,16},{16,24},{24,32},{32,40},{40,48},{48,56},{56,64},{64,7... | collective-permute-start | bytes 835592 | tf_op jit(solution)/shard_map/ppermute | solution.py:32
  20.2 7.7 %collective-permute-start.1 = (f32[4,136,128]{2,1,0:T(8,128)S(1)}, f32[4,136,128]{2,1,0:T(8,128)S(1)}, u32[]{:S(2)}, u32[]{:S(2)}) collective-permute-start(f32[4,136,128]{2,1,0:T(8,128)S(1)} %maximum_maximum_fusion.1), channel_id=1, source_target_pairs={{0,16},{8,24},{16,32},{24,40},{32,48},{40,56},{48,64},{56,72},{64,... | collective-permute-start | bytes 835592 | tf_op jit(solution)/shard_map/ppermute | solution.py:32
  28.1 15.3 %copy-start.7 = (bf16[512]{0:T(512)(128)(2,1)S(1)}, bf16[512]{0:T(512)(128)(2,1)}, u32[]{:S(2)}) copy-start(bf16[512]{0:T(512)(128)(2,1)} %param.25) | copy-start | bytes 3076
  28.2 9.1 %collective-permute-start.2 = (f32[4,136,128]{2,1,0:T(8,128)S(1)}, f32[4,136,128]{2,1,0:T(8,128)S(1)}, u32[]{:S(2)}, u32[]{:S(2)}) collective-permute-start(f32[4,136,128]{2,1,0:T(8,128)S(1)} %maximum_maximum_fusion.2), channel_id=1, source_target_pairs={{0,32},{8,40},{16,48},{24,56},{32,64},{40,72},{48,80},{56,88},{64,... | collective-permute-start | bytes 835592 | tf_op jit(solution)/shard_map/ppermute | solution.py:32
  37.5 9.9 %collective-permute-start.3 = (f32[4,136,128]{2,1,0:T(8,128)S(1)}, f32[4,136,128]{2,1,0:T(8,128)S(1)}, u32[]{:S(2)}, u32[]{:S(2)}) collective-permute-start(f32[4,136,128]{2,1,0:T(8,128)S(1)} %maximum_maximum_fusion.3), channel_id=1, source_target_pairs={{0,64},{8,72},{16,80},{24,88},{32,96},{40,104},{48,112},{56,120},{... | collective-permute-start | bytes 835592 | tf_op jit(solution)/shard_map/ppermute | solution.py:32
  47.7 8.9 %collective-permute-start.4 = (f32[4,136,128]{2,1,0:T(8,128)S(1)}, f32[4,136,128]{2,1,0:T(8,128)S(1)}, u32[]{:S(2)}, u32[]{:S(2)}) collective-permute-start(f32[4,136,128]{2,1,0:T(8,128)S(1)} %maximum_maximum_fusion.4), channel_id=1, source_target_pairs={{0,128},{8,136},{16,144},{24,152},{32,160},{40,168},{48,176},{56,1... | collective-permute-start | bytes 835592 | tf_op jit(solution)/shard_map/ppermute | solution.py:32
  72.8 11.3 %copy-start.8 = (bf16[384]{0:T(512)(128)(2,1)S(1)}, bf16[384]{0:T(512)(128)(2,1)}, u32[]{:S(2)}) copy-start(bf16[384]{0:T(512)(128)(2,1)} %param.28) | copy-start | bytes 2308
  76.9 47.8 %copy-start.3 = (bf16[256,384]{1,0:T(8,128)(2,1)S(1)}, bf16[256,384]{1,0:T(8,128)(2,1)}, u32[]{:S(2)}) copy-start(bf16[256,384]{1,0:T(8,128)(2,1)} %param.27) | copy-start | bytes 589828
  76.9 49.1 %copy-start.6 = (s32[256,2]{0,1:T(2,128)S(1)}, s32[256,2]{0,1:T(2,128)}, u32[]{:S(2)}) copy-start(s32[256,2]{0,1:T(2,128)} %param.30) | copy-start | bytes 6148
  76.9 47.5 %all-to-all-start = ((bf16[8,256,384]{2,1,0:T(8,128)(2,1)}), bf16[8,256,384]{2,1,0:T(8,128)(2,1)S(1)}, u32[]{:S(2)}, u32[]{:S(2)}) async-start(bf16[8,256,384]{2,1,0:T(8,128)(2,1)} %fusion.10), calls=%async_computation | async-start | bytes 3145728 | tf_op jit(solution)/shard_map/all_to_all | solution.py:96
  84.0 72.0 %all-gather.5.cloned.1.call-start = ((), (), s32[]{:S(2)}) async-start(), calls=%async_computation.5 | async-start | bytes 1824768 | tf_op jit(solution)/shard_map/all_gather | solution.py:106
  169.5 68.8 %all-to-all-start.1 = ((bf16[32,24,3072]{2,1,0:T(8,128)(2,1)}), bf16[32,24,3072]{2,1,0:T(8,128)(2,1)}, u32[]{:S(2)}, u32[]{:S(2)}) async-start(bf16[32,24,3072]{2,1,0:T(8,128)(2,1)} %broadcast_select_fusion), calls=%async_computation.1 | async-start | bytes 9437184 | tf_op jit(solution)/shard_map/all_to_all | solution.py:130
  182.2 132.4 %reduce-scatter.2.cloned.1.call-start = ((), (), s32[]{:S(2)}) async-start(), calls=%async_computation.6 | async-start | bytes 5308416 | tf_op jit(solution)/shard_map/reduce_scatter | solution.py:139
  238.3 7.0 %copy-start.9 = (bf16[1,3072,640]{2,1,0:T(8,128)(2,1)S(1)}, bf16[1,3072,640]{2,1,0:T(8,128)(2,1)}, u32[]{:S(2)}) copy-start(bf16[1,3072,640]{2,1,0:T(8,128)(2,1)} %param.32) | copy-start | bytes 11796484
  245.3 6.4 %copy-start.2 = (bf16[80,8,8,384]{3,2,1,0:T(8,128)(2,1)S(1)}, bf16[80,8,8,384]{3,2,1,0:T(8,128)(2,1)}, u32[]{:S(2)}) copy-start(bf16[80,8,8,384]{3,2,1,0:T(8,128)(2,1)} %copy.106) | copy-start | bytes 11796484
  257.2 64.9 %copy-start.5 = (bf16[3072,32]{0,1:T(8,128)(2,1)S(1)}, bf16[3072,32]{0,1:T(8,128)(2,1)}, u32[]{:S(2)}) copy-start(bf16[3072,32]{0,1:T(8,128)(2,1)} %param.29) | copy-start | bytes 589828
  314.6 19.7 %all-to-all-start.2 = ((bf16[32,24,384]{2,1,0:T(8,128)(2,1)}), bf16[32,24,384]{2,1,0:T(8,128)(2,1)S(1)}, u32[]{:S(2)}, u32[]{:S(2)}) async-start(bf16[32,24,384]{2,1,0:T(8,128)(2,1)} %bitcast.130), calls=%async_computation.3 | async-start | bytes 1179648 | tf_op jit(solution)/shard_map/all_to_all | solution.py:141
Sparse Core Ops, SparseCore 0:
  16.6 56.1 all-gather.2
  126.1 29.9 all-gather.4
  257.4 57.1 reduce-scatter.1

commit v2 on v1

--- a/solution.py
+++ b/solution.py
@@ -26,15 +26,21 @@
     identity = jnp.zeros_like(packed).at[:, rows].set(1.0)
     window = packed
     before = identity
-    shift = 1
-    while shift < count:
-        pairs = [(j, j + shift) for j in range(count - shift)]
-        got = lax.ppermute(window, axis, pairs)
-        got = jnp.where(mine >= shift, got, identity)
-        before = combine(got, before)
-        if 2 * shift < count:
-            window = combine(got, window)
-        shift *= 2
+    base = 1
+    while base < count:
+        joined = None
+        for step in range(1, 4):
+            shift = step * base
+            if shift >= count:
+                break
+            pairs = [(j, j + shift) for j in range(count - shift)]
+            got = lax.ppermute(window, axis, pairs)
+            got = jnp.where(mine >= shift, got, identity)
+            joined = got if joined is None else combine(got, joined)
+        before = combine(joined, before)
+        if 4 * base < count:
+            window = combine(joined, window)
+        base *= 4
     return before[:, :rows]
 
 
@@ -92,9 +98,9 @@
     )
     partial_proj = jnp.einsum(
         "tk,gck->gtc", normed, weight_all, preferred_element_type=jnp.float32
-    ).astype(jnp.bfloat16)
-    pieces = lax.all_to_all(partial_proj, "head", 0, 0, tiled=True)
-    stream_mine = residual.astype(jnp.float32) + jnp.sum(pieces.astype(jnp.float32), axis=0)
+    )
+    total = lax.psum_scatter(partial_proj, "head", scatter_dimension=0, tiled=True)
+    stream_mine = residual.astype(jnp.float32) + total[0]
     sq_part = jnp.sum(stream_mine * stream_mine, axis=1)
     sq_hi = sq_part.astype(jnp.bfloat16)
     sq_lo = (sq_part - sq_hi.astype(jnp.float32)).astype(jnp.bfloat16)
@@ -127,18 +133,22 @@
     outgoing = jnp.where(filled[:, None], moe_in[slot_token], blank).reshape(
         experts, capacity, full
     )
-    arriving = lax.all_to_all(outgoing, "ctx", split_axis=0, concat_axis=0, tiled=True)
-    flat = arriving.reshape(-1, full)
-    gate = jnp.dot(flat, gate_weight[0], preferred_element_type=jnp.float32)
-    up = jnp.dot(flat, up_weight[0], preferred_element_type=jnp.float32)
-    activated = (jax.nn.silu(gate) * up).astype(jnp.bfloat16)
+    half = capacity // 2
     down = down_weight[0].reshape(down_weight.shape[1], groups, width)
-    partial_value = jnp.einsum(
-        "rf,fgc->grc", activated, down, preferred_element_type=jnp.float32
-    ).astype(jnp.bfloat16)
-    summed = lax.psum_scatter(partial_value, "head", scatter_dimension=0, tiled=True)
-    summed = summed.reshape(arriving.shape[0], arriving.shape[1], width)
-    returned = lax.all_to_all(summed, "ctx", split_axis=0, concat_axis=0, tiled=True)
+    parts = []
+    for lo, hi in ((0, half), (half, capacity)):
+        arriving = lax.all_to_all(outgoing[:, lo:hi], "ctx", split_axis=0, concat_axis=0, tiled=True)
+        flat = arriving.reshape(-1, full)
+        gate = jnp.dot(flat, gate_weight[0], preferred_element_type=jnp.float32)
+        up = jnp.dot(flat, up_weight[0], preferred_element_type=jnp.float32)
+        activated = (jax.nn.silu(gate) * up).astype(jnp.bfloat16)
+        partial_value = jnp.einsum(
+            "rf,fgc->grc", activated, down, preferred_element_type=jnp.float32
+        ).astype(jnp.bfloat16)
+        summed = lax.psum_scatter(partial_value, "head", scatter_dimension=0, tiled=True)
+        summed = summed.reshape(arriving.shape[0], arriving.shape[1], width)
+        parts.append(lax.all_to_all(summed, "ctx", split_axis=0, concat_axis=0, tiled=True))
+    returned = jnp.concatenate(parts, axis=1)
     picked_rows = returned.reshape(experts * capacity, width)[slot].astype(jnp.float32)
     moe_out = jnp.sum(picked_rows.reshape(rows, TOP, width) * mix_weights[:, :, None], axis=1)
     return stream_mine + moe_out

time: 346 us -> 395 us (1.14)
  blocking collectives: 0 us -> 46.5 us
  waiting for transfers between devices: 216 us -> 179 us
  local copies, waits for them, and re-layouts: 22.9 us -> 39.4 us
  matrix products: 26.3 us -> 39.6 us
  starting transfers between devices: 51.5 us -> 59.1 us
    all_to_all x2 -> x1, waiting for transfers between devices: 91.3 us -> 34.8 us  [on_device(): lax.all_to_all(outgoing[:, lo:hi], 'ctx', split_axis=0, concat_axis=0, ti...]
    all_to_all x0 -> x1, blocking collectives: none -> 46.5 us  [on_device(): lax.all_to_all(outgoing[:, lo:hi], 'ctx', split_axis=0, concat_axis=0, ti...]
    reduce_scatter x0 -> x1, waiting for transfers between devices: none -> 45.2 us  [on_device(): lax.psum_scatter(partial_proj, 'head', scatter_dimension=0, tiled=True)]
    reduce_scatter x1 -> x2, waiting for transfers between devices: 57.3 us -> 27.5 us  [on_device(): lax.psum_scatter(partial_value, 'head', scatter_dimension=0, tiled=True)]
    all_gather x1, waiting for transfers between devices: 15.2 us -> 0.02 us  [on_device(): lax.all_gather(out_weight, 'ctx', axis=0, tiled=True)]
    dot_general x1 -> x2, matrix products: 5.52 us -> 20.6 us  [on_device(): jnp.einsum('rf,fgc->grc', activated, down, preferred_element_type=jnp.flo...]
    ppermute x5 -> x7, waiting for transfers between devices: 18.1 us -> 31.2 us  [exclusive_scan(): got = lax.ppermute(window, axis, pairs)]
    reshape x0 -> x4, local copies, waits for them, and re-layouts: none -> 12 us  [the longest x2 8.47 us: on_device(): flat = arriving.reshape(-1, full)]
  transfers between devices with their start and end apart: 11 -> 15, of which waited for: 11 -> 10; matrix products, arithmetic and copies ran while one was open for 5% -> 12% of each run, Pallas kernels for 0% -> 0%
where the time goes in v2:
time: 395 us; the launch traced here: 394 us
  waiting for transfers between devices  179 us (45%)
  starting transfers between devices  59.1 us (15%)
  blocking collectives  46.5 us (12%)
  matrix products  39.6 us (10%)
  local copies, waits for them, and re-layouts  39.4 us (10%)
  other arithmetic  16.4 us (4%)
  between operations  13.7 us (3%)
    all_to_all x1, blocking collectives, on_device(): lax.all_to_all(outgoing[:, lo:hi], 'ctx', split_axis=0, concat_axis=0, ti...  46.5 us
    reduce_scatter x1, waiting for transfers between devices, on_device(): lax.psum_scatter(partial_proj, 'head', scatter_dimension=0, tiled=True)  45.2 us
    all_to_all x1, waiting for transfers between devices, on_device(): lax.all_to_all(outgoing[:, lo:hi], 'ctx', split_axis=0, concat_axis=0, ti...  34.8 us
    ppermute x7, waiting for transfers between devices, exclusive_scan(): got = lax.ppermute(window, axis, pairs)  31.2 us
    ppermute x7, starting transfers between devices, exclusive_scan(): got = lax.ppermute(window, axis, pairs)  30.6 us
    all_gather x1, waiting for transfers between devices, on_device(): gathered = lax.all_gather(payload, 'head', axis=1, tiled=True)  30 us
    reduce_scatter x2, waiting for transfers between devices, on_device(): lax.psum_scatter(partial_value, 'head', scatter_dimension=0, tiled=True)  27.5 us
    dot_general x2, matrix products, on_device(): jnp.einsum('rf,fgc->grc', activated, down, preferred_element_type=jnp.flo...  20.6 us
  transfers between devices with their start and end apart: 15, of which 10 were waited for; matrix products, arithmetic and copies ran while one was open for 12% of the time, Pallas kernels for 0%

profile of v2, /device:TPU:1, one launch (start us, length us, event | category | flops | bytes accessed | tf_op | source)
XLA Modules:
  0.0 394.2 jit_solution(11019015704431273449)
XLA Ops:
  13.1 6.0 %collective-permute-start.2 = (f32[4,136,128]{2,1,0:T(8,128)S(1)}, f32[4,136,128]{2,1,0:T(8,128)S(1)}, u32[]{:S(2)}, u32[]{:S(2)}) collective-permute-start(f32[4,136,128]{2,1,0:T(8,128)S(1)} %maximum_maximum_fusion), channel_id=1, source_target_pairs={{0,24},{8,32},{16,40},{24,48},{32,56},{40,64},{48,72},{56,80},{64,... | collective-permute-start | bytes 835592 | tf_op jit(solution)/shard_map/ppermute | solution.py:37
  24.3 6.0 %collective-permute-done.1 = f32[4,136,128]{2,1,0:T(8,128)S(1)} collective-permute-done((f32[4,136,128]{2,1,0:T(8,128)S(1)}, f32[4,136,128]{2,1,0:T(8,128)S(1)}, u32[]{:S(2)}, u32[]{:S(2)}) %collective-permute-start.1) | collective-permute-done | bytes 278560 | tf_op jit(solution)/shard_map/ppermute | solution.py:37
  36.4 5.3 %collective-permute-start.5 = (f32[4,136,128]{2,1,0:T(8,128)S(1)}, f32[4,136,128]{2,1,0:T(8,128)S(1)}, u32[]{:S(2)}, u32[]{:S(2)}) collective-permute-start(f32[4,136,128]{2,1,0:T(8,128)S(1)} %maximum_maximum_fusion.1), channel_id=1, source_target_pairs={{0,32},{8,40},{16,48},{24,56},{32,64},{40,72},{48,80},{56,88},{64,... | collective-permute-start | bytes 835592 | tf_op jit(solution)/shard_map/ppermute | solution.py:37
  44.9 6.0 %collective-permute-start.3 = (f32[4,136,128]{2,1,0:T(8,128)S(1)}, f32[4,136,128]{2,1,0:T(8,128)S(1)}, u32[]{:S(2)}, u32[]{:S(2)}) collective-permute-start(f32[4,136,128]{2,1,0:T(8,128)S(1)} %maximum_maximum_fusion.1), channel_id=1, source_target_pairs={{0,96},{8,104},{16,112},{24,120},{32,128},{40,136},{48,144},{56,15... | collective-permute-start | bytes 835592 | tf_op jit(solution)/shard_map/ppermute | solution.py:37
  52.5 15.9 %collective-permute-done.4 = f32[4,136,128]{2,1,0:T(8,128)S(1)} collective-permute-done((f32[4,136,128]{2,1,0:T(8,128)S(1)}, f32[4,136,128]{2,1,0:T(8,128)S(1)}, u32[]{:S(2)}, u32[]{:S(2)}) %collective-permute-start.4) | collective-permute-done | bytes 278560 | tf_op jit(solution)/shard_map/ppermute | solution.py:37
  69.0 5.8 %collective-permute-start.6 = (f32[4,136,128]{2,1,0:T(8,128)S(1)}, f32[4,136,128]{2,1,0:T(8,128)S(1)}, u32[]{:S(2)}, u32[]{:S(2)}) collective-permute-start(f32[4,136,128]{2,1,0:T(8,128)S(1)} %maximum_maximum_fusion.2), channel_id=1, source_target_pairs={{0,128},{8,136},{16,144},{24,152},{32,160},{40,168},{48,176},{56,1... | collective-permute-start | bytes 835592 | tf_op jit(solution)/shard_map/ppermute | solution.py:37
  76.3 4.3 %collective-permute-done.6 = f32[4,136,128]{2,1,0:T(8,128)S(1)} collective-permute-done((f32[4,136,128]{2,1,0:T(8,128)S(1)}, f32[4,136,128]{2,1,0:T(8,128)S(1)}, u32[]{:S(2)}, u32[]{:S(2)}) %collective-permute-start.6) | collective-permute-done | bytes 278560 | tf_op jit(solution)/shard_map/ppermute | solution.py:37
  82.3 4.6 %convolution_bitcast_fusion = f32[8,256,384]{2,1,0:T(8,128)} fusion(bf16[256,512,1]{0,1,2:T(8,128)(2,1)S(1)} %bitcast.159, bf16[8,384,512]{2,1,0:T(8,128)(2,1)} %bitcast.158), kind=kOutput, calls=%fused_computation.20 | convolution fusion | flops 805306368 | bytes 6553600 | tf_op jit(solution)/shard_map/tk,gck->gtc/dot_general | solution.py:99
  87.6 45.2 %reduce-scatter.4.cloned.1.call-done = f32[1,256,384]{2,1,0:T(8,128)} async-done(((f32[8,256,384]{2,1,0:T(8,128)}), f32[1,256,384]{2,1,0:T(8,128)}) %reduce-scatter.4.cloned.1.call-update) | async-done | bytes 393232 | tf_op jit(solution)/shard_map/reduce_scatter | solution.py:102
  142.7 30.0 %all-gather.5.cloned.1.call-done = bf16[264,3072]{1,0:T(8,128)(2,1)} async-done(((bf16[264,384]{1,0:T(8,128)(2,1)}), bf16[264,3072]{1,0:T(8,128)(2,1)}) %all-gather.5.cloned.1.call-update) | async-done | bytes 1622032 | tf_op jit(solution)/shard_map/all_gather | solution.py:112
  176.3 5.0 %gather_fusion = bf16[768,3072]{1,0:T(8,128)(2,1)} fusion(bf16[256,3072]{1,0:T(8,128)(2,1)S(1)} %multiply_convert_fusion, s32[1024]{0:T(1024)S(1)} %pad_clamp_fusion.1), kind=kCustom, calls=%fused_computation | custom fusion | bytes 9440256 | tf_op jit(solution)/shard_map/gather | solution.py:133
  188.0 12.7 %all-to-all-start.2 = ((bf16[32,12,3072]{2,1,0:T(8,128)(2,1)}), bf16[32,12,3072]{2,1,0:T(8,128)(2,1)}, u32[]{:S(2)}, u32[]{:S(2)}) async-start(bf16[32,12,3072]{2,1,0:T(8,128)(2,1)} %get-tuple-element.66), calls=%async_computation.4 | async-start | bytes 6291456 | tf_op jit(solution)/shard_map/all_to_all | solution.py:140
  200.8 4.9 %copy.111 = bf16[80,8,8,384]{3,2,1,0:T(8,128)(2,1)} copy(bf16[80,8,8,384]{3,1,2,0:T(8,128)(2,1)} %bitcast.155) | data formatting | bytes 7864320
  205.7 34.8 %all-to-all-done.2 = bf16[32,12,3072]{2,1,0:T(8,128)(2,1)} async-done(((bf16[32,12,3072]{2,1,0:T(8,128)(2,1)}), bf16[32,12,3072]{2,1,0:T(8,128)(2,1)}, u32[]{:S(2)}, u32[]{:S(2)}) %all-to-all-start.2) | async-done | bytes 2359328 | tf_op jit(solution)/shard_map/all_to_all | solution.py:140
  240.6 4.2 %reshape.300 = bf16[384,3072]{1,0:T(8,128)(2,1)} reshape(bf16[32,12,3072]{2,1,0:T(8,128)(2,1)} %all-to-all-done.2) | data formatting | bytes 4718592 | tf_op jit(solution)/shard_map/reshape | solution.py:141
  244.8 4.8 %fusion.4 = f32[384,640]{1,0:T(8,128)S(1)} fusion(bf16[384,3072]{1,0:T(8,128)(2,1)} %reshape.300, bf16[1,3072,640]{2,1,0:T(8,128)(2,1)} %param.31), kind=kOutput, calls=%fused_computation.9 | convolution fusion | flops 1509949440 | bytes 7274496 | tf_op jit(solution)/shard_map/dot_general | solution.py:142
  249.6 10.3 %convert_bitcast_fusion = bf16[8,384,384]{2,1,0:T(8,128)(2,1)} fusion(bf16[640,8,384]{2,1,0:T(8,128)(2,1)} %bitcast.156, bf16[384,3072]{1,0:T(8,128)(2,1)} %reshape.300, bf16[1,3072,640]{2,1,0:T(8,128)(2,1)} %param.32, f32[384,640]{1,0:T(8,128)S(1)} %fusion.4), kind=kOutput, calls=%fused_computation.18 | convolution fusion | flops 3022553088 | bytes 13565952 | tf_op jit(solution)/shard_map/rf,fgc->grc/dot_general | solution.py:145
  260.0 46.5 %all_to_all.20 = bf16[32,12,3072]{2,1,0:T(8,128)(2,1)} all-to-all(bf16[32,12,3072]{2,1,0:T(8,128)(2,1)} %get-tuple-element.65), channel_id=1, replica_groups=mesh['ctx'=32,'head'=8] {'ctx'}, dimensions={0} | all-to-all | bytes 4718592 | tf_op jit(solution)/shard_map/all_to_all | solution.py:140
  306.5 4.2 %reshape.298 = bf16[384,3072]{1,0:T(8,128)(2,1)} reshape(bf16[32,12,3072]{2,1,0:T(8,128)(2,1)} %all_to_all.20) | data formatting | bytes 4718592 | tf_op jit(solution)/shard_map/reshape | solution.py:141
  310.8 4.8 %fusion.6 = f32[384,640]{1,0:T(8,128)S(1)} fusion(bf16[384,3072]{1,0:T(8,128)(2,1)} %reshape.298, bf16[1,3072,640]{2,1,0:T(8,128)(2,1)} %param.31), kind=kOutput, calls=%fused_computation.11 | convolution fusion | flops 1509949440 | bytes 7274496 | tf_op jit(solution)/shard_map/dot_general | solution.py:142
  315.6 10.3 %convert_bitcast_fusion.1 = bf16[8,384,384]{2,1,0:T(8,128)(2,1)} fusion(bf16[640,8,384]{2,1,0:T(8,128)(2,1)} %bitcast.157, bf16[384,3072]{1,0:T(8,128)(2,1)} %reshape.298, bf16[1,3072,640]{2,1,0:T(8,128)(2,1)} %param.32, f32[384,640]{1,0:T(8,128)S(1)} %fusion.6), kind=kOutput, calls=%fused_computation.19 | convolution fusion | flops 3022553088 | bytes 13565952 | tf_op jit(solution)/shard_map/rf,fgc->grc/dot_general | solution.py:145
  332.3 27.5 %reduce-scatter.6.cloned.1.call-done = bf16[1,384,384]{2,1,0:T(8,128)(2,1)} async-done(((bf16[8,384,384]{2,1,0:T(8,128)(2,1)}), bf16[1,384,384]{2,1,0:T(8,128)(2,1)}) %reduce-scatter.6.cloned.1.call-update) | async-done | bytes 294928 | tf_op jit(solution)/shard_map/reduce_scatter | solution.py:148
  361.5 11.7 %all-to-all-start.1 = ((bf16[32,12,384]{2,1,0:T(8,128)(2,1)}), bf16[32,12,384]{2,1,0:T(8,128)(2,1)S(1)}, u32[]{:S(2)}, u32[]{:S(2)}) async-start(bf16[32,12,384]{2,1,0:T(8,128)(2,1)} %reshape.299), calls=%async_computation.3 | async-start | bytes 786432 | tf_op jit(solution)/shard_map/all_to_all | solution.py:150
  373.5 9.9 %all-to-all-done.1 = bf16[32,12,384]{2,1,0:T(8,128)(2,1)S(1)} async-done(((bf16[32,12,384]{2,1,0:T(8,128)(2,1)}), bf16[32,12,384]{2,1,0:T(8,128)(2,1)S(1)}, u32[]{:S(2)}, u32[]{:S(2)}) %all-to-all-start.1) | async-done | bytes 294944 | tf_op jit(solution)/shard_map/all_to_all | solution.py:150
  (135 shorter events, 59.4 us)
Async XLA Ops:
  6.5 44.4 %copy-start = (bf16[256,512]{1,0:T(8,128)(2,1)S(1)}, bf16[256,512]{1,0:T(8,128)(2,1)}, u32[]{:S(2)}) copy-start(bf16[256,512]{1,0:T(8,128)(2,1)} %param.21) | copy-start | bytes 786436
  6.5 44.5 %copy-start.5 = (bf16[256,512]{1,0:T(8,128)(2,1)S(1)}, bf16[256,512]{1,0:T(8,128)(2,1)}, u32[]{:S(2)}) copy-start(bf16[256,512]{1,0:T(8,128)(2,1)} %param.23) | copy-start | bytes 786436
  6.5 75.8 %all-gather.3.cloned.1.call-start = ((), (), s32[]{:S(2)}) async-start(), calls=%async_computation.7 | async-start | bytes 3244032 | tf_op jit(solution)/shard_map/all_gather | solution.py:96
  7.3 125.6 %reduce-scatter.4.cloned.1.call-start = ((), (), s32[]{:S(2)}) async-start(), calls=%async_computation.8 | async-start | bytes 3538944 | tf_op jit(solution)/shard_map/reduce_scatter | solution.py:102
  10.8 25.5 %copy-start.10 = (f32[136]{0:T(256)}, f32[136]{0:T(256)S(1)}, u32[]{:S(2)}) copy-start(f32[136]{0:T(256)S(1)} %pad.23.clone) | copy-start | bytes 1636
  13.1 11.2 %collective-permute-start.2 = (f32[4,136,128]{2,1,0:T(8,128)S(1)}, f32[4,136,128]{2,1,0:T(8,128)S(1)}, u32[]{:S(2)}, u32[]{:S(2)}) collective-permute-start(f32[4,136,128]{2,1,0:T(8,128)S(1)} %maximum_maximum_fusion), channel_id=1, source_target_pairs={{0,24},{8,32},{16,40},{24,48},{32,56},{40,64},{48,72},{56,80},{64,... | collective-permute-start | bytes 835592 | tf_op jit(solution)/shard_map/ppermute | solution.py:37
  19.2 11.2 %collective-permute-start.1 = (f32[4,136,128]{2,1,0:T(8,128)S(1)}, f32[4,136,128]{2,1,0:T(8,128)S(1)}, u32[]{:S(2)}, u32[]{:S(2)}) collective-permute-start(f32[4,136,128]{2,1,0:T(8,128)S(1)} %maximum_maximum_fusion), channel_id=1, source_target_pairs={{0,8},{8,16},{16,24},{24,32},{32,40},{40,48},{48,56},{56,64},{64,7... | collective-permute-start | bytes 835592 | tf_op jit(solution)/shard_map/ppermute | solution.py:37
  21.1 13.3 %collective-permute-start = (f32[4,136,128]{2,1,0:T(8,128)S(1)}, f32[4,136,128]{2,1,0:T(8,128)S(1)}, u32[]{:S(2)}, u32[]{:S(2)}) collective-permute-start(f32[4,136,128]{2,1,0:T(8,128)S(1)} %maximum_maximum_fusion), channel_id=1, source_target_pairs={{0,16},{8,24},{16,32},{24,40},{32,48},{40,56},{48,64},{56,72},{64,... | collective-permute-start | bytes 835592 | tf_op jit(solution)/shard_map/ppermute | solution.py:37
  35.4 33.0 %copy-start.2 = (f32[4,136,128]{2,1,0:T(8,128)S(1)}, f32[4,136,128]{2,1,0:T(8,128)}, u32[]{:S(2)}) copy-start(f32[4,136,128]{2,1,0:T(8,128)} %constant.174.clone.1) | copy-start | bytes 835588
  36.0 8.9 %copy-start.7 = (f32[4,1,128]{2,1,0:T(1,128)}, f32[4,1,128]{2,1,0:T(1,128)S(1)}, u32[]{:S(2)}) copy-start(f32[4,1,128]{2,1,0:T(1,128)S(1)} %get-tuple-element.62) | copy-start | bytes 6148
  36.4 16.2 %collective-permute-start.5 = (f32[4,136,128]{2,1,0:T(8,128)S(1)}, f32[4,136,128]{2,1,0:T(8,128)S(1)}, u32[]{:S(2)}, u32[]{:S(2)}) collective-permute-start(f32[4,136,128]{2,1,0:T(8,128)S(1)} %maximum_maximum_fusion.1), channel_id=1, source_target_pairs={{0,32},{8,40},{16,48},{24,56},{32,64},{40,72},{48,80},{56,88},{64,... | collective-permute-start | bytes 835592 | tf_op jit(solution)/shard_map/ppermute | solution.py:37
  41.7 26.7 %collective-permute-start.4 = (f32[4,136,128]{2,1,0:T(8,128)S(1)}, f32[4,136,128]{2,1,0:T(8,128)S(1)}, u32[]{:S(2)}, u32[]{:S(2)}) collective-permute-start(f32[4,136,128]{2,1,0:T(8,128)S(1)} %maximum_maximum_fusion.1), channel_id=1, source_target_pairs={{0,64},{8,72},{16,80},{24,88},{32,96},{40,104},{48,112},{56,120},{... | collective-permute-start | bytes 835592 | tf_op jit(solution)/shard_map/ppermute | solution.py:37
  44.9 23.5 %collective-permute-start.3 = (f32[4,136,128]{2,1,0:T(8,128)S(1)}, f32[4,136,128]{2,1,0:T(8,128)S(1)}, u32[]{:S(2)}, u32[]{:S(2)}) collective-permute-start(f32[4,136,128]{2,1,0:T(8,128)S(1)} %maximum_maximum_fusion.1), channel_id=1, source_target_pairs={{0,96},{8,104},{16,112},{24,120},{32,128},{40,136},{48,144},{56,15... | collective-permute-start | bytes 835592 | tf_op jit(solution)/shard_map/ppermute | solution.py:37
  52.4 16.5 %copy-start.11 = (f32[136]{0:T(256)S(1)}, f32[136]{0:T(256)}, u32[]{:S(2)}) copy-start(f32[136]{0:T(256)} %copy-done.10) | copy-start | bytes 1636
  69.0 11.6 %collective-permute-start.6 = (f32[4,136,128]{2,1,0:T(8,128)S(1)}, f32[4,136,128]{2,1,0:T(8,128)S(1)}, u32[]{:S(2)}, u32[]{:S(2)}) collective-permute-start(f32[4,136,128]{2,1,0:T(8,128)S(1)} %maximum_maximum_fusion.2), channel_id=1, source_target_pairs={{0,128},{8,136},{16,144},{24,152},{32,160},{40,168},{48,176},{56,1... | collective-permute-start | bytes 835592 | tf_op jit(solution)/shard_map/ppermute | solution.py:37
  87.0 45.9 %copy-start.4 = (bf16[256,384]{1,0:T(8,128)(2,1)S(1)}, bf16[256,384]{1,0:T(8,128)(2,1)}, u32[]{:S(2)}) copy-start(bf16[256,384]{1,0:T(8,128)(2,1)} %param.27) | copy-start | bytes 589828
  87.0 48.2 %copy-start.9 = (s32[256,2]{0,1:T(2,128)S(1)}, s32[256,2]{0,1:T(2,128)}, u32[]{:S(2)}) copy-start(s32[256,2]{0,1:T(2,128)} %param.30) | copy-start | bytes 6148
  87.0 85.8 %all-gather.5.cloned.1.call-start = ((), (), s32[]{:S(2)}) async-start(), calls=%async_computation.9 | async-start | bytes 1824768 | tf_op jit(solution)/shard_map/all_gather | solution.py:112
  188.0 52.5 %all-to-all-start.2 = ((bf16[32,12,3072]{2,1,0:T(8,128)(2,1)}), bf16[32,12,3072]{2,1,0:T(8,128)(2,1)}, u32[]{:S(2)}, u32[]{:S(2)}) async-start(bf16[32,12,3072]{2,1,0:T(8,128)(2,1)} %get-tuple-element.66), calls=%async_computation.4 | async-start | bytes 6291456 | tf_op jit(solution)/shard_map/all_to_all | solution.py:140
  200.7 125.2 %reduce-scatter.8.cloned.1.call-start = ((), (), s32[]{:S(2)}) async-start(), calls=%async_computation.11 | async-start | bytes 2654208 | tf_op jit(solution)/shard_map/reduce_scatter | solution.py:148
  259.9 99.8 %reduce-scatter.6.cloned.1.call-start = ((), (), s32[]{:S(2)}) async-start(), calls=%async_computation.10 | async-start | bytes 2654208 | tf_op jit(solution)/shard_map/reduce_scatter | solution.py:148
  325.9 5.8 %copy-start.6 = (bf16[3072,32]{0,1:T(8,128)(2,1)S(1)}, bf16[3072,32]{0,1:T(8,128)(2,1)}, u32[]{:S(2)}) copy-start(bf16[3072,32]{0,1:T(8,128)(2,1)} %param.29) | copy-start | bytes 589828
  327.7 33.8 %all-to-all-start.3 = ((bf16[32,12,384]{2,1,0:T(8,128)(2,1)}), bf16[32,12,384]{2,1,0:T(8,128)(2,1)S(1)}, u32[]{:S(2)}, u32[]{:S(2)}) async-start(bf16[32,12,384]{2,1,0:T(8,128)(2,1)} %reshape.301), calls=%async_computation.6 | async-start | bytes 786432 | tf_op jit(solution)/shard_map/all_to_all | solution.py:150
  361.5 21.8 %all-to-all-start.1 = ((bf16[32,12,384]{2,1,0:T(8,128)(2,1)}), bf16[32,12,384]{2,1,0:T(8,128)(2,1)S(1)}, u32[]{:S(2)}, u32[]{:S(2)}) async-start(bf16[32,12,384]{2,1,0:T(8,128)(2,1)} %reshape.299), calls=%async_computation.3 | async-start | bytes 786432 | tf_op jit(solution)/shard_map/all_to_all | solution.py:150
  (5 other events, 13.0 us)
Sparse Core Ops, SparseCore 0:
  9.9 61.5 all-gather.2
  87.1 45.7 reduce-scatter.3
  135.3 37.3 all-gather.4
  260.0 34.8 reduce-scatter.7
  326.0 33.6 reduce-scatter.5

commit v3 on v1

--- a/solution.py
+++ b/solution.py
@@ -93,8 +93,8 @@
     partial_proj = jnp.einsum(
         "tk,gck->gtc", normed, weight_all, preferred_element_type=jnp.float32
     ).astype(jnp.bfloat16)
-    pieces = lax.all_to_all(partial_proj, "head", 0, 0, tiled=True)
-    stream_mine = residual.astype(jnp.float32) + jnp.sum(pieces.astype(jnp.float32), axis=0)
+    total = lax.psum_scatter(partial_proj, "head", scatter_dimension=0, tiled=True)
+    stream_mine = residual.astype(jnp.float32) + total[0].astype(jnp.float32)
     sq_part = jnp.sum(stream_mine * stream_mine, axis=1)
     sq_hi = sq_part.astype(jnp.bfloat16)
     sq_lo = (sq_part - sq_hi.astype(jnp.float32)).astype(jnp.bfloat16)
@@ -121,12 +121,9 @@
     position = jnp.sum(before * onehot, axis=1)
     slot = flat_ids * capacity + position
     owner = jnp.arange(rows * TOP, dtype=jnp.int32) // TOP
-    slot_token = jnp.zeros((experts * capacity,), jnp.int32).at[slot].set(owner)
-    filled = jnp.zeros((experts * capacity,), jnp.bool_).at[slot].set(True)
-    blank = jnp.zeros((), jnp.bfloat16)
-    outgoing = jnp.where(filled[:, None], moe_in[slot_token], blank).reshape(
-        experts, capacity, full
-    )
+    slot_token = jnp.full((experts * capacity,), rows, jnp.int32).at[slot].set(owner)
+    padded = jnp.concatenate([moe_in, jnp.zeros((8, full), jnp.bfloat16)], axis=0)
+    outgoing = padded[slot_token].reshape(experts, capacity, full)
     arriving = lax.all_to_all(outgoing, "ctx", split_axis=0, concat_axis=0, tiled=True)
     flat = arriving.reshape(-1, full)
     gate = jnp.dot(flat, gate_weight[0], preferred_element_type=jnp.float32)

time: 346 us -> 339 us (0.980)
  waiting for transfers between devices: 216 us -> 223 us
  starting transfers between devices: 51.5 us -> 44.6 us
  other arithmetic: 14.6 us -> 10.5 us
    all_to_all x1 -> x0, waiting for transfers between devices: 40.3 us -> none  [on_device(): pieces = lax.all_to_all(partial_proj, 'head', 0, 0, tiled=True)]
    reduce_scatter x0 -> x1, waiting for transfers between devices: none -> 37 us  [on_device(): lax.psum_scatter(partial_proj, 'head', scatter_dimension=0, tiled=True)]
    all_gather x1, waiting for transfers between devices: 22.7 us -> 32.9 us  [on_device(): gathered = lax.all_gather(payload, 'head', axis=1, tiled=True)]
    all_to_all x1 -> x0, starting transfers between devices: 7.12 us -> none  [on_device(): pieces = lax.all_to_all(partial_proj, 'head', 0, 0, tiled=True)]
    select_n x3 -> x2, other arithmetic: 4.86 us -> 0.01 us  [the longest x1 0.01 us: on_device(): jnp.full((experts * capacity,), rows, jnp.int32).at[slot].set(owner)]
  transfers between devices with their start and end apart: 11 -> 11, of which waited for: 11 -> 11; matrix products, arithmetic and copies ran while one was open for 5% -> 4% of each run, Pallas kernels for 0% -> 0%
where the time goes in v3:
time: 339 us; the launch traced here: 338 us
  waiting for transfers between devices  223 us (66%)
  starting transfers between devices  44.6 us (13%)
  matrix products  26.3 us (8%)
  local copies, waits for them, and re-layouts  20.5 us (6%)
  between operations  13.7 us (4%)
  other arithmetic  10.5 us (3%)
    reduce_scatter x1, waiting for transfers between devices, on_device(): lax.psum_scatter(partial_value, 'head', scatter_dimension=0, tiled=True)  57.3 us
    all_to_all x1, waiting for transfers between devices, on_device(): lax.all_to_all(outgoing, 'ctx', split_axis=0, concat_axis=0, tiled=True)  50.8 us
    reduce_scatter x1, waiting for transfers between devices, on_device(): lax.psum_scatter(partial_proj, 'head', scatter_dimension=0, tiled=True)  37 us
    all_gather x1, waiting for transfers between devices, on_device(): gathered = lax.all_gather(payload, 'head', axis=1, tiled=True)  32.9 us
    ppermute x5, starting transfers between devices, exclusive_scan(): got = lax.ppermute(window, axis, pairs)  24.1 us
    ppermute x5, waiting for transfers between devices, exclusive_scan(): got = lax.ppermute(window, axis, pairs)  18 us
    all_gather x1, waiting for transfers between devices, on_device(): lax.all_gather(out_weight, 'ctx', axis=0, tiled=True)  15.2 us
    all_to_all x1, starting transfers between devices, on_device(): lax.all_to_all(outgoing, 'ctx', split_axis=0, concat_axis=0, tiled=True)  12.7 us
  transfers between devices with their start and end apart: 11, of which 11 were waited for; matrix products, arithmetic and copies ran while one was open for 4% of the time, Pallas kernels for 0%

profile of v3, /device:TPU:1, one launch (start us, length us, event | category | flops | bytes accessed | tf_op | source)
XLA Modules:
  0.0 338.2 jit_solution(921708857383462036)
XLA Ops:
  11.9 4.5 %collective-permute-start = (f32[4,136,128]{2,1,0:T(8,128)S(1)}, f32[4,136,128]{2,1,0:T(8,128)S(1)}, u32[]{:S(2)}, u32[]{:S(2)}) collective-permute-start(f32[4,136,128]{2,1,0:T(8,128)S(1)} %maximum_maximum_fusion), channel_id=1, source_target_pairs={{0,8},{8,16},{16,24},{24,32},{32,40},{40,48},{48,56},{56,64},{64,7... | collective-permute-start | bytes 835592 | tf_op jit(solution)/shard_map/ppermute | solution.py:32
  16.5 3.4 %collective-permute-done = f32[4,136,128]{2,1,0:T(8,128)S(1)} collective-permute-done((f32[4,136,128]{2,1,0:T(8,128)S(1)}, f32[4,136,128]{2,1,0:T(8,128)S(1)}, u32[]{:S(2)}, u32[]{:S(2)}) %collective-permute-start) | collective-permute-done | bytes 278560 | tf_op jit(solution)/shard_map/ppermute | solution.py:32
  20.2 3.1 collective-permute-start.1
  23.5 4.4 %collective-permute-done.1 = f32[4,136,128]{2,1,0:T(8,128)S(1)} collective-permute-done((f32[4,136,128]{2,1,0:T(8,128)S(1)}, f32[4,136,128]{2,1,0:T(8,128)S(1)}, u32[]{:S(2)}, u32[]{:S(2)}) %collective-permute-start.1) | collective-permute-done | bytes 278560 | tf_op jit(solution)/shard_map/ppermute | solution.py:32
  28.2 5.1 %collective-permute-start.2 = (f32[4,136,128]{2,1,0:T(8,128)S(1)}, f32[4,136,128]{2,1,0:T(8,128)S(1)}, u32[]{:S(2)}, u32[]{:S(2)}) collective-permute-start(f32[4,136,128]{2,1,0:T(8,128)S(1)} %maximum_maximum_fusion.2), channel_id=1, source_target_pairs={{0,32},{8,40},{16,48},{24,56},{32,64},{40,72},{48,80},{56,88},{64,... | collective-permute-start | bytes 835592 | tf_op jit(solution)/shard_map/ppermute | solution.py:32
  34.1 3.2 collective-permute-done.2
  37.5 5.9 %collective-permute-start.3 = (f32[4,136,128]{2,1,0:T(8,128)S(1)}, f32[4,136,128]{2,1,0:T(8,128)S(1)}, u32[]{:S(2)}, u32[]{:S(2)}) collective-permute-start(f32[4,136,128]{2,1,0:T(8,128)S(1)} %maximum_maximum_fusion.3), channel_id=1, source_target_pairs={{0,64},{8,72},{16,80},{24,88},{32,96},{40,104},{48,112},{56,120},{... | collective-permute-start | bytes 835592 | tf_op jit(solution)/shard_map/ppermute | solution.py:32
  43.6 3.9 %collective-permute-done.3 = f32[4,136,128]{2,1,0:T(8,128)S(1)} collective-permute-done((f32[4,136,128]{2,1,0:T(8,128)S(1)}, f32[4,136,128]{2,1,0:T(8,128)S(1)}, u32[]{:S(2)}, u32[]{:S(2)}) %collective-permute-start.3) | collective-permute-done | bytes 278560 | tf_op jit(solution)/shard_map/ppermute | solution.py:32
  47.7 5.4 %collective-permute-start.4 = (f32[4,136,128]{2,1,0:T(8,128)S(1)}, f32[4,136,128]{2,1,0:T(8,128)S(1)}, u32[]{:S(2)}, u32[]{:S(2)}) collective-permute-start(f32[4,136,128]{2,1,0:T(8,128)S(1)} %maximum_maximum_fusion.4), channel_id=1, source_target_pairs={{0,128},{8,136},{16,144},{24,152},{32,160},{40,168},{48,176},{56,1... | collective-permute-start | bytes 835592 | tf_op jit(solution)/shard_map/ppermute | solution.py:32
  53.5 3.1 collective-permute-done.4
  57.6 15.2 %all-gather.3.cloned.1.call-done = bf16[3072,512]{1,0:T(8,128)(2,1)} async-done(((bf16[96,512]{1,0:T(8,128)(2,1)}), bf16[3072,512]{1,0:T(8,128)(2,1)}) %all-gather.3.cloned.1.call-update) | async-done | bytes 3145744 | tf_op jit(solution)/shard_map/all_gather | solution.py:90
  72.8 4.1 %fusion.10 = bf16[8,256,384]{2,1,0:T(8,128)(2,1)} fusion(bf16[256,512,1]{0,1,2:T(8,128)(2,1)S(1)} %bitcast.131, bf16[8,384,512]{2,1,0:T(8,128)(2,1)} %bitcast.130), kind=kOutput, calls=%fused_computation.13 | convolution fusion | flops 806092800 | bytes 4980736 | tf_op jit(solution)/shard_map/tk,gck->gtc/dot_general | solution.py:93
  77.0 37.0 %reduce-scatter.3.cloned.1.call-done = bf16[1,256,384]{2,1,0:T(8,128)(2,1)} async-done(((bf16[8,256,384]{2,1,0:T(8,128)(2,1)}), bf16[1,256,384]{2,1,0:T(8,128)(2,1)}) %reduce-scatter.3.cloned.1.call-update) | async-done | bytes 196624 | tf_op jit(solution)/shard_map/reduce_scatter | solution.py:96
  121.1 32.9 %all-gather.5.cloned.1.call-done = bf16[264,3072]{1,0:T(8,128)(2,1)} async-done(((bf16[264,384]{1,0:T(8,128)(2,1)}), bf16[264,3072]{1,0:T(8,128)(2,1)}) %all-gather.5.cloned.1.call-update) | async-done | bytes 1622032 | tf_op jit(solution)/shard_map/all_gather | solution.py:106
  157.7 5.1 %gather_fusion = bf16[768,3072]{1,0:T(8,128)(2,1)} fusion(bf16[264,3072]{1,0:T(8,128)(2,1)S(1)} %concatenate.35, s32[1024]{0:T(1024)S(1)} %pad_clamp_fusion.1), kind=kCustom, calls=%fused_computation | custom fusion | bytes 9440256 | tf_op jit(solution)/shard_map/gather | solution.py:126
  162.8 12.7 %all-to-all-start = ((bf16[32,24,3072]{2,1,0:T(8,128)(2,1)}), bf16[32,24,3072]{2,1,0:T(8,128)(2,1)}, u32[]{:S(2)}, u32[]{:S(2)}) async-start(bf16[32,24,3072]{2,1,0:T(8,128)(2,1)} %bitcast.127), calls=%async_computation.1 | async-start | bytes 9437184 | tf_op jit(solution)/shard_map/all_to_all | solution.py:127
  175.7 5.0 %copy.106 = bf16[80,8,8,384]{3,2,1,0:T(8,128)(2,1)} copy(bf16[80,8,8,384]{3,1,2,0:T(8,128)(2,1)} %bitcast.128) | data formatting | bytes 7864320
  180.7 50.8 %all-to-all-done = bf16[32,24,3072]{2,1,0:T(8,128)(2,1)} async-done(((bf16[32,24,3072]{2,1,0:T(8,128)(2,1)}), bf16[32,24,3072]{2,1,0:T(8,128)(2,1)}, u32[]{:S(2)}, u32[]{:S(2)}) %all-to-all-start) | async-done | bytes 4718624 | tf_op jit(solution)/shard_map/all_to_all | solution.py:127
  231.5 7.0 %fusion.2 = f32[768,640]{1,0:T(8,128)S(1)} fusion(bf16[768,3072]{1,0:T(8,128)(2,1)} %bitcast.17, bf16[1,3072,640]{2,1,0:T(8,128)(2,1)} %param.31), kind=kOutput, calls=%fused_computation.6 | convolution fusion | flops 3019898880 | bytes 10616832 | tf_op jit(solution)/shard_map/dot_general | solution.py:129
  238.5 6.4 %fusion.11 = bf16[768,640,1]{1,0,2:T(8,128)(2,1)S(1)} fusion(bf16[768,3072]{1,0:T(8,128)(2,1)} %bitcast.17, bf16[1,3072,640]{2,1,0:T(8,128)(2,1)S(1)} %copy-done.11, f32[768,640]{1,0:T(8,128)S(1)} %fusion.2), kind=kOutput, calls=%fused_computation.15 | convolution fusion | flops 3022848000 | bytes 11599872 | tf_op jit(solution)/shard_map/dot_general | solution.py:130
  244.9 5.5 %convert_bitcast_fusion = bf16[8,768,384]{2,1,0:T(8,128)(2,1)} fusion(bf16[768,640,1]{1,0,2:T(8,128)(2,1)S(1)} %fusion.11, bf16[640,8,384]{2,1,0:T(8,128)(2,1)S(1)} %bitcast.129), kind=kOutput, calls=%fused_computation.3 | convolution fusion | flops 3022258176 | bytes 9633792 | tf_op jit(solution)/shard_map/rf,fgc->grc/dot_general | solution.py:133
  250.5 57.3 %reduce-scatter.5.cloned.1.call-done = bf16[1,768,384]{2,1,0:T(8,128)(2,1)} async-done(((bf16[8,768,384]{2,1,0:T(8,128)(2,1)}), bf16[1,768,384]{2,1,0:T(8,128)(2,1)}) %reduce-scatter.5.cloned.1.call-update) | async-done | bytes 589840 | tf_op jit(solution)/shard_map/reduce_scatter | solution.py:136
  307.8 7.6 %all-to-all-start.1 = ((bf16[32,24,384]{2,1,0:T(8,128)(2,1)}), bf16[32,24,384]{2,1,0:T(8,128)(2,1)S(1)}, u32[]{:S(2)}, u32[]{:S(2)}) async-start(bf16[32,24,384]{2,1,0:T(8,128)(2,1)} %bitcast.134), calls=%async_computation.3 | async-start | bytes 1179648 | tf_op jit(solution)/shard_map/all_to_all | solution.py:138
  316.3 11.2 %all-to-all-done.1 = bf16[32,24,384]{2,1,0:T(8,128)(2,1)S(1)} async-done(((bf16[32,24,384]{2,1,0:T(8,128)(2,1)}), bf16[32,24,384]{2,1,0:T(8,128)(2,1)S(1)}, u32[]{:S(2)}, u32[]{:S(2)}) %all-to-all-start.1) | async-done | bytes 589856 | tf_op jit(solution)/shard_map/all_to_all | solution.py:138
  (120 shorter events, 24.6 us)
Async XLA Ops:
  6.5 26.8 %copy-start = (bf16[256,512]{1,0:T(8,128)(2,1)S(1)}, bf16[256,512]{1,0:T(8,128)(2,1)}, u32[]{:S(2)}) copy-start(bf16[256,512]{1,0:T(8,128)(2,1)} %param.21) | copy-start | bytes 786436
  6.5 21.4 %copy-start.1 = (f32[4,136,128]{2,1,0:T(8,128)S(1)}, f32[4,136,128]{2,1,0:T(8,128)}, u32[]{:S(2)}) copy-start(f32[4,136,128]{2,1,0:T(8,128)} %constant.171.clone.1) | copy-start | bytes 835588
  6.5 66.2 %all-gather.3.cloned.1.call-start = ((), (), s32[]{:S(2)}) async-start(), calls=%async_computation.4 | async-start | bytes 3244032 | tf_op jit(solution)/shard_map/all_gather | solution.py:90
  9.2 24.2 %copy-start.6 = (bf16[256,512]{1,0:T(8,128)(2,1)S(1)}, bf16[256,512]{1,0:T(8,128)(2,1)}, u32[]{:S(2)}) copy-start(bf16[256,512]{1,0:T(8,128)(2,1)} %param.23) | copy-start | bytes 786436
  11.9 8.0 %collective-permute-start = (f32[4,136,128]{2,1,0:T(8,128)S(1)}, f32[4,136,128]{2,1,0:T(8,128)S(1)}, u32[]{:S(2)}, u32[]{:S(2)}) collective-permute-start(f32[4,136,128]{2,1,0:T(8,128)S(1)} %maximum_maximum_fusion), channel_id=1, source_target_pairs={{0,8},{8,16},{16,24},{24,32},{32,40},{40,48},{48,56},{56,64},{64,7... | collective-permute-start | bytes 835592 | tf_op jit(solution)/shard_map/ppermute | solution.py:32
  16.4 97.6 %reduce-scatter.3.cloned.1.call-start = ((), (), s32[]{:S(2)}) async-start(), calls=%async_computation.5 | async-start | bytes 1769472 | tf_op jit(solution)/shard_map/reduce_scatter | solution.py:96
  20.2 7.7 %collective-permute-start.1 = (f32[4,136,128]{2,1,0:T(8,128)S(1)}, f32[4,136,128]{2,1,0:T(8,128)S(1)}, u32[]{:S(2)}, u32[]{:S(2)}) collective-permute-start(f32[4,136,128]{2,1,0:T(8,128)S(1)} %maximum_maximum_fusion.1), channel_id=1, source_target_pairs={{0,16},{8,24},{16,32},{24,40},{32,48},{40,56},{48,64},{56,72},{64,... | collective-permute-start | bytes 835592 | tf_op jit(solution)/shard_map/ppermute | solution.py:32
  28.1 15.3 %copy-start.9 = (bf16[512]{0:T(512)(128)(2,1)S(1)}, bf16[512]{0:T(512)(128)(2,1)}, u32[]{:S(2)}) copy-start(bf16[512]{0:T(512)(128)(2,1)} %param.25) | copy-start | bytes 3076
  28.2 9.1 %collective-permute-start.2 = (f32[4,136,128]{2,1,0:T(8,128)S(1)}, f32[4,136,128]{2,1,0:T(8,128)S(1)}, u32[]{:S(2)}, u32[]{:S(2)}) collective-permute-start(f32[4,136,128]{2,1,0:T(8,128)S(1)} %maximum_maximum_fusion.2), channel_id=1, source_target_pairs={{0,32},{8,40},{16,48},{24,56},{32,64},{40,72},{48,80},{56,88},{64,... | collective-permute-start | bytes 835592 | tf_op jit(solution)/shard_map/ppermute | solution.py:32
  37.5 9.9 %collective-permute-start.3 = (f32[4,136,128]{2,1,0:T(8,128)S(1)}, f32[4,136,128]{2,1,0:T(8,128)S(1)}, u32[]{:S(2)}, u32[]{:S(2)}) collective-permute-start(f32[4,136,128]{2,1,0:T(8,128)S(1)} %maximum_maximum_fusion.3), channel_id=1, source_target_pairs={{0,64},{8,72},{16,80},{24,88},{32,96},{40,104},{48,112},{56,120},{... | collective-permute-start | bytes 835592 | tf_op jit(solution)/shard_map/ppermute | solution.py:32
  47.7 8.9 %collective-permute-start.4 = (f32[4,136,128]{2,1,0:T(8,128)S(1)}, f32[4,136,128]{2,1,0:T(8,128)S(1)}, u32[]{:S(2)}, u32[]{:S(2)}) collective-permute-start(f32[4,136,128]{2,1,0:T(8,128)S(1)} %maximum_maximum_fusion.4), channel_id=1, source_target_pairs={{0,128},{8,136},{16,144},{24,152},{32,160},{40,168},{48,176},{56,1... | collective-permute-start | bytes 835592 | tf_op jit(solution)/shard_map/ppermute | solution.py:32
  72.8 4.2 %copy-start.10 = (bf16[384]{0:T(512)(128)(2,1)S(1)}, bf16[384]{0:T(512)(128)(2,1)}, u32[]{:S(2)}) copy-start(bf16[384]{0:T(512)(128)(2,1)} %param.28) | copy-start | bytes 2308
  72.8 41.2 %copy-start.3 = (bf16[256,384]{1,0:T(8,128)(2,1)S(1)}, bf16[256,384]{1,0:T(8,128)(2,1)}, u32[]{:S(2)}) copy-start(bf16[256,384]{1,0:T(8,128)(2,1)} %param.27) | copy-start | bytes 589828
  72.8 43.5 %copy-start.8 = (s32[256,2]{0,1:T(2,128)S(1)}, s32[256,2]{0,1:T(2,128)}, u32[]{:S(2)}) copy-start(s32[256,2]{0,1:T(2,128)} %param.30) | copy-start | bytes 6148
  76.9 77.1 %all-gather.5.cloned.1.call-start = ((), (), s32[]{:S(2)}) async-start(), calls=%async_computation.6 | async-start | bytes 1824768 | tf_op jit(solution)/shard_map/all_gather | solution.py:106
  162.8 68.8 %all-to-all-start = ((bf16[32,24,3072]{2,1,0:T(8,128)(2,1)}), bf16[32,24,3072]{2,1,0:T(8,128)(2,1)}, u32[]{:S(2)}, u32[]{:S(2)}) async-start(bf16[32,24,3072]{2,1,0:T(8,128)(2,1)} %bitcast.127), calls=%async_computation.1 | async-start | bytes 9437184 | tf_op jit(solution)/shard_map/all_to_all | solution.py:127
  175.5 132.3 %reduce-scatter.5.cloned.1.call-start = ((), (), s32[]{:S(2)}) async-start(), calls=%async_computation.7 | async-start | bytes 5308416 | tf_op jit(solution)/shard_map/reduce_scatter | solution.py:136
  231.5 7.0 %copy-start.11 = (bf16[1,3072,640]{2,1,0:T(8,128)(2,1)S(1)}, bf16[1,3072,640]{2,1,0:T(8,128)(2,1)}, u32[]{:S(2)}) copy-start(bf16[1,3072,640]{2,1,0:T(8,128)(2,1)} %param.32) | copy-start | bytes 11796484
  238.5 6.4 %copy-start.2 = (bf16[80,8,8,384]{3,2,1,0:T(8,128)(2,1)S(1)}, bf16[80,8,8,384]{3,2,1,0:T(8,128)(2,1)}, u32[]{:S(2)}) copy-start(bf16[80,8,8,384]{3,2,1,0:T(8,128)(2,1)} %copy.106) | copy-start | bytes 11796484
  250.5 65.0 %copy-start.7 = (bf16[3072,32]{0,1:T(8,128)(2,1)S(1)}, bf16[3072,32]{0,1:T(8,128)(2,1)}, u32[]{:S(2)}) copy-start(bf16[3072,32]{0,1:T(8,128)(2,1)} %param.29) | copy-start | bytes 589828
  307.8 19.7 %all-to-all-start.1 = ((bf16[32,24,384]{2,1,0:T(8,128)(2,1)}), bf16[32,24,384]{2,1,0:T(8,128)(2,1)S(1)}, u32[]{:S(2)}, u32[]{:S(2)}) async-start(bf16[32,24,384]{2,1,0:T(8,128)(2,1)} %bitcast.134), calls=%async_computation.3 | async-start | bytes 1179648 | tf_op jit(solution)/shard_map/all_to_all | solution.py:138
  316.0 14.9 %copy-start.4 = (bf16[256,384]{1,0:T(8,128)(2,1)S(1)}, bf16[256,384]{1,0:T(8,128)(2,1)}, u32[]{:S(2)}) copy-start(bf16[256,384]{1,0:T(8,128)(2,1)} %param.27) | copy-start | bytes 589828
  316.0 14.9 %copy-start.5 = (bf16[1,256,384]{2,1,0:T(8,128)(2,1)S(1)}, bf16[1,256,384]{2,1,0:T(8,128)(2,1)}, u32[]{:S(2)}) copy-start(bf16[1,256,384]{2,1,0:T(8,128)(2,1)} %reduce-scatter.3.cloned.1.call-done) | copy-start | bytes 589828
Sparse Core Ops, SparseCore 0:
  16.6 56.1 all-gather.2
  77.0 36.9 reduce-scatter.2
  116.4 37.5 all-gather.4
  250.6 57.1 reduce-scatter.4

commit v4 on v3

--- a/solution.py
+++ b/solution.py
@@ -87,28 +87,23 @@
     )
     width = residual.shape[1]
     full = width * groups
-    weight_all = lax.all_gather(out_weight, "ctx", axis=0, tiled=True).reshape(
-        groups, width, heads_here * HEAD_DIM
+    weight_all = lax.all_gather(out_weight, "ctx", axis=0, tiled=True)
+    partial_proj = lax.dot_general(
+        normed, weight_all, (((1,), (1,)), ((), ())), preferred_element_type=jnp.float32
     )
-    partial_proj = jnp.einsum(
-        "tk,gck->gtc", normed, weight_all, preferred_element_type=jnp.float32
-    ).astype(jnp.bfloat16)
-    total = lax.psum_scatter(partial_proj, "head", scatter_dimension=0, tiled=True)
-    stream_mine = residual.astype(jnp.float32) + total[0].astype(jnp.float32)
-    sq_part = jnp.sum(stream_mine * stream_mine, axis=1)
-    sq_hi = sq_part.astype(jnp.bfloat16)
-    sq_lo = (sq_part - sq_hi.astype(jnp.float32)).astype(jnp.bfloat16)
-    extra = jnp.zeros((8, width), jnp.bfloat16)
-    extra = extra.at[0].set(norm_gain)
-    extra = extra.at[1, :rows].set(sq_hi)
-    extra = extra.at[2, :rows].set(sq_lo)
-    payload = jnp.concatenate([stream_mine.astype(jnp.bfloat16), extra], axis=0)
-    gathered = lax.all_gather(payload, "head", axis=1, tiled=True)
-    stream_wide = gathered[:rows].astype(jnp.float32)
-    gain_full = gathered[rows].astype(jnp.float32)
-    sq_parts = gathered[rows + 1 : rows + 3].astype(jnp.float32).reshape(2, groups, width)
-    stream_sq = jnp.sum(sq_parts[:, :, :rows], axis=(0, 1))[:, None] / full
+    mine = lax.axis_index("head")
+    own = (jnp.arange(full) // width) == mine
+    resid_wide = jnp.tile(residual.astype(jnp.float32), (1, groups))
+    partial_proj = jnp.where(own[None, :], partial_proj + resid_wide, partial_proj)
+    gain_wide = jnp.where(own, jnp.tile(norm_gain, groups), jnp.zeros((), jnp.bfloat16))
+    extra = jnp.zeros((8, full), jnp.bfloat16).at[0].set(gain_wide)
+    payload = jnp.concatenate([partial_proj.astype(jnp.bfloat16), extra], axis=0)
+    summed_all = lax.psum(payload, "head")
+    stream_wide = summed_all[:rows].astype(jnp.float32)
+    gain_full = summed_all[rows].astype(jnp.float32)
+    stream_sq = jnp.mean(stream_wide * stream_wide, axis=-1, keepdims=True)
     moe_in = (stream_wide * lax.rsqrt(stream_sq + EPSILON) * gain_full).astype(jnp.bfloat16)
+    stream_mine = lax.dynamic_slice_in_dim(stream_wide, mine * width, width, 1)
     experts = router.shape[1]
     capacity = 3 * rows * TOP // (2 * experts)
     logits = jnp.dot(moe_in, router, preferred_element_type=jnp.float32)

time: 339 us -> 339 us (level)
  waiting for transfers between devices: 223 us -> 214 us
  other arithmetic: 10.5 us -> 16.3 us
    psum x0 -> x1, waiting for transfers between devices: none -> 70.8 us  [on_device(): summed_all = lax.psum(payload, 'head')]
    all_gather x2 -> x1, waiting for transfers between devices: 48.1 us -> 9.79 us  [on_device(): weight_all = lax.all_gather(out_weight, 'ctx', axis=0, tiled=True)]
    reduce_scatter x1 -> x0, waiting for transfers between devices: 37 us -> none  [on_device(): lax.psum_scatter(partial_proj, 'head', scatter_dimension=0, tiled=True)]
    unnamed x28 -> x44, local copies, waits for them, and re-layouts: 5.24 us -> 7.22 us
  transfers between devices with their start and end apart: 11 -> 10, of which waited for: 11 -> 10; matrix products, arithmetic and copies ran while one was open for 4% -> 6% of each run, Pallas kernels for 0% -> 0%
where the time goes in v4:
time: 339 us; the launch traced here: 338 us
  waiting for transfers between devices  214 us (63%)
  starting transfers between devices  45.4 us (13%)
  matrix products  27.1 us (8%)
  local copies, waits for them, and re-layouts  21.5 us (6%)
  other arithmetic  16.3 us (5%)
  between operations  13.7 us (4%)
    psum x1, waiting for transfers between devices, on_device(): summed_all = lax.psum(payload, 'head')  70.8 us
    reduce_scatter x1, waiting for transfers between devices, on_device(): lax.psum_scatter(partial_value, 'head', scatter_dimension=0, tiled=True)  56.1 us
    all_to_all x1, waiting for transfers between devices, on_device(): lax.all_to_all(outgoing, 'ctx', split_axis=0, concat_axis=0, tiled=True)  50.8 us
    ppermute x5, starting transfers between devices, exclusive_scan(): got = lax.ppermute(window, axis, pairs)  25.9 us
    ppermute x5, waiting for transfers between devices, exclusive_scan(): got = lax.ppermute(window, axis, pairs)  16.8 us
    all_to_all x1, starting transfers between devices, on_device(): lax.all_to_all(outgoing, 'ctx', split_axis=0, concat_axis=0, tiled=True)  11.6 us
    all_to_all x1, waiting for transfers between devices, on_device(): lax.all_to_all(summed, 'ctx', split_axis=0, concat_axis=0, tiled=True)  10.1 us
    all_gather x1, waiting for transfers between devices, on_device(): weight_all = lax.all_gather(out_weight, 'ctx', axis=0, tiled=True)  9.79 us
  transfers between devices with their start and end apart: 10, of which 10 were waited for; matrix products, arithmetic and copies ran while one was open for 6% of the time, Pallas kernels for 0%

profile of v4, /device:TPU:1, one launch (start us, length us, event | category | flops | bytes accessed | tf_op | source)
XLA Modules:
  0.0 338.4 jit_solution(15149927439564802497)
XLA Ops:
  11.9 4.5 %collective-permute-start = (f32[4,136,128]{2,1,0:T(8,128)S(1)}, f32[4,136,128]{2,1,0:T(8,128)S(1)}, u32[]{:S(2)}, u32[]{:S(2)}) collective-permute-start(f32[4,136,128]{2,1,0:T(8,128)S(1)} %maximum_maximum_fusion), channel_id=1, source_target_pairs={{0,8},{8,16},{16,24},{24,32},{32,40},{40,48},{48,56},{56,64},{64,7... | collective-permute-start | bytes 835592 | tf_op jit(solution)/shard_map/ppermute | solution.py:32
  17.2 2.7 collective-permute-done
  20.2 3.1 collective-permute-start.1
  23.5 4.4 %collective-permute-done.1 = f32[4,136,128]{2,1,0:T(8,128)S(1)} collective-permute-done((f32[4,136,128]{2,1,0:T(8,128)S(1)}, f32[4,136,128]{2,1,0:T(8,128)S(1)}, u32[]{:S(2)}, u32[]{:S(2)}) %collective-permute-start.1) | collective-permute-done | bytes 278560 | tf_op jit(solution)/shard_map/ppermute | solution.py:32
  28.3 5.1 %collective-permute-start.2 = (f32[4,136,128]{2,1,0:T(8,128)S(1)}, f32[4,136,128]{2,1,0:T(8,128)S(1)}, u32[]{:S(2)}, u32[]{:S(2)}) collective-permute-start(f32[4,136,128]{2,1,0:T(8,128)S(1)} %maximum_maximum_fusion.2), channel_id=1, source_target_pairs={{0,32},{8,40},{16,48},{24,56},{32,64},{40,72},{48,80},{56,88},{64,... | collective-permute-start | bytes 835592 | tf_op jit(solution)/shard_map/ppermute | solution.py:32
  34.9 2.5 collective-permute-done.2
  39.0 6.6 %collective-permute-start.3 = (f32[4,136,128]{2,1,0:T(8,128)}, f32[4,136,128]{2,1,0:T(8,128)}, u32[]{:S(2)}, u32[]{:S(2)}) collective-permute-start(f32[4,136,128]{2,1,0:T(8,128)} %maximum_maximum_fusion.3), channel_id=1, source_target_pairs={{0,64},{8,72},{16,80},{24,88},{32,96},{40,104},{48,112},{56,120},{... | collective-permute-start | bytes 835592 | tf_op jit(solution)/shard_map/ppermute | solution.py:32
  46.6 2.1 collective-permute-done.3
  49.0 6.6 %collective-permute-start.4 = (f32[4,136,128]{2,1,0:T(8,128)S(1)}, f32[4,136,128]{2,1,0:T(8,128)S(1)}, u32[]{:S(2)}, u32[]{:S(2)}) collective-permute-start(f32[4,136,128]{2,1,0:T(8,128)S(1)} %maximum_maximum_fusion.4), channel_id=1, source_target_pairs={{0,128},{8,136},{16,144},{24,152},{32,160},{40,168},{48,176},{56,1... | collective-permute-start | bytes 835592 | tf_op jit(solution)/shard_map/ppermute | solution.py:32
  55.9 5.2 %collective-permute-done.4 = f32[4,136,128]{2,1,0:T(8,128)S(1)} collective-permute-done((f32[4,136,128]{2,1,0:T(8,128)S(1)}, f32[4,136,128]{2,1,0:T(8,128)S(1)}, u32[]{:S(2)}, u32[]{:S(2)}) %collective-permute-start.4) | collective-permute-done | bytes 278560 | tf_op jit(solution)/shard_map/ppermute | solution.py:32
  62.8 9.8 %all-gather.2.cloned.1.call-done = bf16[3072,512]{1,0:T(8,128)(2,1)} async-done(((bf16[96,512]{1,0:T(8,128)(2,1)}), bf16[3072,512]{1,0:T(8,128)(2,1)}) %all-gather.2.cloned.1.call-update) | async-done | bytes 3145744 | tf_op jit(solution)/shard_map/all_gather | solution.py:90
  72.6 3.0 fusion.7
  79.3 2.4 scatter_custom_fusion
  81.8 70.8 %all-reduce.4.cloned.1.call-done = bf16[264,3072]{1,0:T(8,128)(2,1)} async-done(((bf16[264,3072]{1,0:T(8,128)(2,1)}), bf16[264,3072]{1,0:T(8,128)(2,1)}) %all-reduce.4.cloned.1.call-update) | async-done | bytes 1622032 | tf_op jit(solution)/shard_map/psum | solution.py:101
  157.3 5.1 %gather_fusion = bf16[768,3072]{1,0:T(8,128)(2,1)} fusion(bf16[264,3072]{1,0:T(8,128)(2,1)S(1)} %concatenate.31, s32[1024]{0:T(1024)S(1)} %pad_clamp_fusion.1), kind=kCustom, calls=%fused_computation | custom fusion | bytes 9440256 | tf_op jit(solution)/shard_map/gather | solution.py:121
  162.4 11.6 %all-to-all-start = ((bf16[32,24,3072]{2,1,0:T(8,128)(2,1)}), bf16[32,24,3072]{2,1,0:T(8,128)(2,1)}, u32[]{:S(2)}, u32[]{:S(2)}) async-start(bf16[32,24,3072]{2,1,0:T(8,128)(2,1)} %bitcast.117), calls=%async_computation | async-start | bytes 9437184 | tf_op jit(solution)/shard_map/all_to_all | solution.py:122
  174.2 5.0 %copy.100 = bf16[80,8,8,384]{3,2,1,0:T(8,128)(2,1)} copy(bf16[80,8,8,384]{3,1,2,0:T(8,128)(2,1)} %bitcast.120) | data formatting | bytes 7864320
  179.2 50.8 %all-to-all-done = bf16[32,24,3072]{2,1,0:T(8,128)(2,1)} async-done(((bf16[32,24,3072]{2,1,0:T(8,128)(2,1)}), bf16[32,24,3072]{2,1,0:T(8,128)(2,1)}, u32[]{:S(2)}, u32[]{:S(2)}) %all-to-all-start) | async-done | bytes 4718624 | tf_op jit(solution)/shard_map/all_to_all | solution.py:122
  230.1 7.0 %fusion.2 = f32[768,640]{1,0:T(8,128)S(1)} fusion(bf16[768,3072]{1,0:T(8,128)(2,1)} %bitcast.12, bf16[1,3072,640]{2,1,0:T(8,128)(2,1)} %param.27), kind=kOutput, calls=%fused_computation.7 | convolution fusion | flops 3019898880 | bytes 10616832 | tf_op jit(solution)/shard_map/dot_general | solution.py:124
  237.1 6.4 %fusion.13 = bf16[768,640,1]{1,0,2:T(8,128)(2,1)S(1)} fusion(bf16[768,3072]{1,0:T(8,128)(2,1)} %bitcast.12, bf16[1,3072,640]{2,1,0:T(8,128)(2,1)S(1)} %copy-done.18, f32[768,640]{1,0:T(8,128)S(1)} %fusion.2), kind=kOutput, calls=%fused_computation.20 | convolution fusion | flops 3022848000 | bytes 11599872 | tf_op jit(solution)/shard_map/dot_general | solution.py:125
  243.5 5.5 %convert_bitcast_fusion = bf16[8,768,384]{2,1,0:T(8,128)(2,1)} fusion(bf16[768,640,1]{1,0,2:T(8,128)(2,1)S(1)} %fusion.13, bf16[640,8,384]{2,1,0:T(8,128)(2,1)S(1)} %bitcast.121), kind=kOutput, calls=%fused_computation.4 | convolution fusion | flops 3022258176 | bytes 9633792 | tf_op jit(solution)/shard_map/rf,fgc->grc/dot_general | solution.py:128
  250.9 56.1 %reduce-scatter.2.cloned.1.call-done = bf16[1,768,384]{2,1,0:T(8,128)(2,1)} async-done(((bf16[8,768,384]{2,1,0:T(8,128)(2,1)}), bf16[1,768,384]{2,1,0:T(8,128)(2,1)}) %reduce-scatter.2.cloned.1.call-update) | async-done | bytes 589840 | tf_op jit(solution)/shard_map/reduce_scatter | solution.py:131
  307.0 7.6 %all-to-all-start.1 = ((bf16[32,24,384]{2,1,0:T(8,128)(2,1)}), bf16[32,24,384]{2,1,0:T(8,128)(2,1)S(1)}, u32[]{:S(2)}, u32[]{:S(2)}) async-start(bf16[32,24,384]{2,1,0:T(8,128)(2,1)} %bitcast.125), calls=%async_computation.2 | async-start | bytes 1179648 | tf_op jit(solution)/shard_map/all_to_all | solution.py:133
  316.7 10.1 %all-to-all-done.1 = bf16[32,24,384]{2,1,0:T(8,128)(2,1)S(1)} async-done(((bf16[32,24,384]{2,1,0:T(8,128)(2,1)}), bf16[32,24,384]{2,1,0:T(8,128)(2,1)S(1)}, u32[]{:S(2)}, u32[]{:S(2)}) %all-to-all-start.1) | async-done | bytes 589856 | tf_op jit(solution)/shard_map/all_to_all | solution.py:133
  (129 shorter events, 30.7 us)
Async XLA Ops:
  6.5 26.8 %copy-start = (bf16[256,512]{1,0:T(8,128)(2,1)S(1)}, bf16[256,512]{1,0:T(8,128)(2,1)}, u32[]{:S(2)}) copy-start(bf16[256,512]{1,0:T(8,128)(2,1)} %param.17) | copy-start | bytes 786436
  6.5 21.4 %copy-start.2 = (f32[4,136,128]{2,1,0:T(8,128)S(1)}, f32[4,136,128]{2,1,0:T(8,128)}, u32[]{:S(2)}) copy-start(f32[4,136,128]{2,1,0:T(8,128)} %constant.131.clone.1) | copy-start | bytes 835588
  6.5 66.1 %all-gather.2.cloned.1.call-start = ((), (), s32[]{:S(2)}) async-start(), calls=%async_computation.3 | async-start | bytes 3244032 | tf_op jit(solution)/shard_map/all_gather | solution.py:90
  9.2 24.2 %copy-start.14 = (bf16[256,512]{1,0:T(8,128)(2,1)S(1)}, bf16[256,512]{1,0:T(8,128)(2,1)}, u32[]{:S(2)}) copy-start(bf16[256,512]{1,0:T(8,128)(2,1)} %param.19) | copy-start | bytes 786436
  11.9 8.0 %collective-permute-start = (f32[4,136,128]{2,1,0:T(8,128)S(1)}, f32[4,136,128]{2,1,0:T(8,128)S(1)}, u32[]{:S(2)}, u32[]{:S(2)}) collective-permute-start(f32[4,136,128]{2,1,0:T(8,128)S(1)} %maximum_maximum_fusion), channel_id=1, source_target_pairs={{0,8},{8,16},{16,24},{24,32},{32,40},{40,48},{48,56},{56,64},{64,7... | collective-permute-start | bytes 835592 | tf_op jit(solution)/shard_map/ppermute | solution.py:32
  16.4 136.2 %all-reduce.4.cloned.1.call-start = ((), (), s32[]{:S(2)}) async-start(), calls=%async_computation.4 | async-start | bytes 3244032 | tf_op jit(solution)/shard_map/psum | solution.py:101
  19.9 17.4 %copy-start.5 = (f32[4,136,128]{2,1,0:T(8,128)}, f32[4,136,128]{2,1,0:T(8,128)S(1)}, u32[]{:S(2)}) copy-start(f32[4,136,128]{2,1,0:T(8,128)S(1)} %broadcast_select_fusion.1) | copy-start | bytes 835588
  20.2 7.7 %collective-permute-start.1 = (f32[4,136,128]{2,1,0:T(8,128)S(1)}, f32[4,136,128]{2,1,0:T(8,128)S(1)}, u32[]{:S(2)}, u32[]{:S(2)}) collective-permute-start(f32[4,136,128]{2,1,0:T(8,128)S(1)} %maximum_maximum_fusion.1), channel_id=1, source_target_pairs={{0,16},{8,24},{16,32},{24,40},{32,48},{40,56},{48,64},{56,72},{64,... | collective-permute-start | bytes 835592 | tf_op jit(solution)/shard_map/ppermute | solution.py:32
  28.0 11.0 %copy-start.9 = (f32[4,136,128]{2,1,0:T(8,128)}, f32[4,136,128]{2,1,0:T(8,128)S(1)}, u32[]{:S(2)}) copy-start(f32[4,136,128]{2,1,0:T(8,128)S(1)} %broadcast_select_fusion.2) | copy-start | bytes 835588
  28.2 17.5 %copy-start.17 = (bf16[512]{0:T(512)(128)(2,1)S(1)}, bf16[512]{0:T(512)(128)(2,1)}, u32[]{:S(2)}) copy-start(bf16[512]{0:T(512)(128)(2,1)} %param.21) | copy-start | bytes 3076
  28.2 17.5 %copy-start.15 = (bf16[256,384]{1,0:T(8,128)(2,1)S(1)}, bf16[256,384]{1,0:T(8,128)(2,1)}, u32[]{:S(2)}) copy-start(bf16[256,384]{1,0:T(8,128)(2,1)} %param.23) | copy-start | bytes 589828
  28.3 9.1 %collective-permute-start.2 = (f32[4,136,128]{2,1,0:T(8,128)S(1)}, f32[4,136,128]{2,1,0:T(8,128)S(1)}, u32[]{:S(2)}, u32[]{:S(2)}) collective-permute-start(f32[4,136,128]{2,1,0:T(8,128)S(1)} %maximum_maximum_fusion.2), channel_id=1, source_target_pairs={{0,32},{8,40},{16,48},{24,56},{32,64},{40,72},{48,80},{56,88},{64,... | collective-permute-start | bytes 835592 | tf_op jit(solution)/shard_map/ppermute | solution.py:32
  37.4 8.3 %copy-start.11 = (f32[4,136,128]{2,1,0:T(8,128)}, f32[4,136,128]{2,1,0:T(8,128)S(1)}, u32[]{:S(2)}) copy-start(f32[4,136,128]{2,1,0:T(8,128)S(1)} %broadcast_select_fusion) | copy-start | bytes 835588
  39.0 9.7 %collective-permute-start.3 = (f32[4,136,128]{2,1,0:T(8,128)}, f32[4,136,128]{2,1,0:T(8,128)}, u32[]{:S(2)}, u32[]{:S(2)}) collective-permute-start(f32[4,136,128]{2,1,0:T(8,128)} %maximum_maximum_fusion.3), channel_id=1, source_target_pairs={{0,64},{8,72},{16,80},{24,88},{32,96},{40,104},{48,112},{56,120},{... | collective-permute-start | bytes 835592 | tf_op jit(solution)/shard_map/ppermute | solution.py:32
  45.9 9.7 %copy-start.6 = (f32[4,136,128]{2,1,0:T(8,128)S(1)}, f32[4,136,128]{2,1,0:T(8,128)}, u32[]{:S(2)}) copy-start(f32[4,136,128]{2,1,0:T(8,128)} %copy-done.5) | copy-start | bytes 835588
  45.9 15.2 %copy-start.10 = (f32[4,136,128]{2,1,0:T(8,128)S(1)}, f32[4,136,128]{2,1,0:T(8,128)}, u32[]{:S(2)}) copy-start(f32[4,136,128]{2,1,0:T(8,128)} %copy-done.9) | copy-start | bytes 835588
  45.9 15.2 %copy-start.12 = (f32[4,136,128]{2,1,0:T(8,128)S(1)}, f32[4,136,128]{2,1,0:T(8,128)}, u32[]{:S(2)}) copy-start(f32[4,136,128]{2,1,0:T(8,128)} %copy-done.11) | copy-start | bytes 835588
  45.9 15.2 %copy-start.13 = (f32[256,4,128]{0,2,1:T(8,128)S(1)}, f32[256,4,128]{0,2,1:T(8,128)}, u32[]{:S(2)}) copy-start(f32[256,4,128]{0,2,1:T(8,128)} %convolution_bitcast_fusion.1) | copy-start | bytes 1572868
  49.0 12.2 %collective-permute-start.4 = (f32[4,136,128]{2,1,0:T(8,128)S(1)}, f32[4,136,128]{2,1,0:T(8,128)S(1)}, u32[]{:S(2)}, u32[]{:S(2)}) collective-permute-start(f32[4,136,128]{2,1,0:T(8,128)S(1)} %maximum_maximum_fusion.4), channel_id=1, source_target_pairs={{0,128},{8,136},{16,144},{24,152},{32,160},{40,168},{48,176},{56,1... | collective-permute-start | bytes 835592 | tf_op jit(solution)/shard_map/ppermute | solution.py:32
  162.4 67.7 %all-to-all-start = ((bf16[32,24,3072]{2,1,0:T(8,128)(2,1)}), bf16[32,24,3072]{2,1,0:T(8,128)(2,1)}, u32[]{:S(2)}, u32[]{:S(2)}) async-start(bf16[32,24,3072]{2,1,0:T(8,128)(2,1)} %bitcast.117), calls=%async_computation | async-start | bytes 9437184 | tf_op jit(solution)/shard_map/all_to_all | solution.py:122
  174.0 133.1 %reduce-scatter.2.cloned.1.call-start = ((), (), s32[]{:S(2)}) async-start(), calls=%async_computation.5 | async-start | bytes 5308416 | tf_op jit(solution)/shard_map/reduce_scatter | solution.py:131
  230.1 7.0 %copy-start.18 = (bf16[1,3072,640]{2,1,0:T(8,128)(2,1)S(1)}, bf16[1,3072,640]{2,1,0:T(8,128)(2,1)}, u32[]{:S(2)}) copy-start(bf16[1,3072,640]{2,1,0:T(8,128)(2,1)} %param.28) | copy-start | bytes 11796484
  249.0 65.6 %copy-start.1 = (bf16[264,3072]{1,0:T(8,128)(2,1)S(1)}, bf16[264,3072]{1,0:T(8,128)(2,1)}, u32[]{:S(2)}) copy-start(bf16[264,3072]{1,0:T(8,128)(2,1)} %all-reduce.4.cloned.1.call-done) | copy-start | bytes 4866052
  307.0 19.7 %all-to-all-start.1 = ((bf16[32,24,384]{2,1,0:T(8,128)(2,1)}), bf16[32,24,384]{2,1,0:T(8,128)(2,1)S(1)}, u32[]{:S(2)}, u32[]{:S(2)}) async-start(bf16[32,24,384]{2,1,0:T(8,128)(2,1)} %bitcast.125), calls=%async_computation.2 | async-start | bytes 1179648 | tf_op jit(solution)/shard_map/all_to_all | solution.py:133
  (5 other events, 14.2 us)
Sparse Core Ops, SparseCore 0:
  16.6 56.0 all-gather.1
  77.1 75.4 all-reduce.3
  249.1 57.8 reduce-scatter.1
